TPU v7x, 128 devices: a whole 4x4x4 slice. The times are simulated.
128 devices in a mesh: dp: 8 (over z, x_lo), ctx: 16 (over y, x_hi, core).
Axes of the slice: x: 4 (x_hi: 2, x_lo: 2; x = x_hi * 2 + x_lo), y: 4, z: 4, core: 2. Of those that a mesh axis runs over, the one named last changes fastest.
Arguments:
- tokens: bfloat16 [8, 262144, 128], P('dp', 'ctx'), may hold values from -6 to 6
- cotangent: bfloat16 [8, 262144, 128], P('dp', 'ctx'), may hold values from -6 to 6
- w_gate_value: bfloat16 [128, 256], replicated, may hold values from -0.5 to 0.5
- w_first: bfloat16 [512, 512], replicated, may hold values from -0.25 to 0.25
- w_second: bfloat16 [512, 512], replicated, may hold values from -0.25 to 0.25
- w_up: bfloat16 [128, 256], replicated, may hold values from -0.5 to 0.5
- w_down: bfloat16 [256, 128], replicated, may hold values from -0.375 to 0.375
Outputs:
- output: bfloat16 [8, 262144, 128], P('dp', 'ctx')
- grad_tokens: bfloat16 [8, 262144, 128], P('dp', 'ctx')
- grad_gate_value: float32 [128, 256], replicated
- grad_first: float32 [512, 512], replicated
- grad_second: float32 [512, 512], replicated
- grad_up: float32 [128, 256], replicated
- grad_down: float32 [256, 128], replicated
All inputs are finite; a program needn't handle non-finite values.
Results may differ from a plain program's by a relative error of at most 0.014.
Values may be sent and summed in bfloat16 or wider, within the bound.
No kernel may reach another device: no remote copies, remote signals or barrier semaphores. Data moves between devices by JAX's collectives and lax.ppermute only.
A program may use at most 256 MiB of HBM per device.

v0:
```python
import jax
import jax.numpy as jnp
from jax import lax
from jax.experimental import pallas as pl
from jax.experimental.pallas import tpu as pltpu
from jax.sharding import PartitionSpec as P

CHUNKS = 1


def silu_slope(pre):
    sigma = jax.nn.sigmoid(pre)
    return sigma * (1.0 + pre * (1.0 - sigma))


def mlp_kernel(x_ref, c_ref, m_ref, wg_ref, wu_ref, wd_ref, wut_ref, wdt_ref,
               out_ref, dh_ref, dm_ref, dg_ref, gu_ref, gd_ref):
    f32 = jnp.float32
    bf16 = jnp.bfloat16
    @pl.when(pl.program_id(0) == 0)
    def _():
        gu_ref[...] = jnp.zeros_like(gu_ref)
        gd_ref[...] = jnp.zeros_like(gd_ref)
    gate = jax.nn.sigmoid(jnp.dot(x_ref[...], wg_ref[...], preferred_element_type=f32))
    mixed32 = m_ref[...].astype(f32)
    cot = c_ref[...]
    hidden = (x_ref[...].astype(f32) + gate * mixed32).astype(bf16)
    pre = jnp.dot(hidden, wu_ref[...], preferred_element_type=f32)
    sigma = jax.nn.sigmoid(pre)
    activated = (pre * sigma).astype(bf16)
    out_ref[...] = (hidden.astype(f32) + jnp.dot(activated, wd_ref[...], preferred_element_type=f32)).astype(bf16)
    gd_ref[...] += jnp.dot(activated.T, cot, preferred_element_type=f32)
    slope = sigma * (1.0 + pre * (1.0 - sigma))
    d_act = (jnp.dot(cot, wdt_ref[...], preferred_element_type=f32) * slope).astype(bf16)
    gu_ref[...] += jnp.dot(hidden.T, d_act, preferred_element_type=f32)
    d_hidden = (cot.astype(f32) + jnp.dot(d_act, wut_ref[...], preferred_element_type=f32)).astype(bf16)
    dh_ref[...] = d_hidden
    dh32 = d_hidden.astype(f32)
    dm_ref[...] = (dh32 * gate).astype(bf16)
    dg_ref[...] = (dh32 * mixed32 * gate * (1.0 - gate)).astype(bf16)

def mlp(x, cot, mixed, w_gate, w_up, w_down, tile=1024):
    rows, width = x.shape
    ff = w_up.shape[1]
    f32 = jnp.float32
    bf16 = jnp.bfloat16
    row = pl.BlockSpec((tile, width), lambda i: (i, 0))
    whole = lambda shape: pl.BlockSpec(shape, lambda i: (0, 0))
    return pl.pallas_call(
        mlp_kernel,
        grid=(rows // tile,),
        in_specs=[row, row, row, whole((width, width)), whole((width, ff)), whole((ff, width)), whole((ff, width)),
                  whole((width, ff))],
        out_specs=[row, row, row, row, whole((width, ff)), whole((ff, width))],
        out_shape=[jax.ShapeDtypeStruct((rows, width), bf16)] * 4 + [jax.ShapeDtypeStruct((width, ff), f32),
                   jax.ShapeDtypeStruct((ff, width), f32)],
        compiler_params=pltpu.CompilerParams(dimension_semantics=("arbitrary",)),
    )(x, cot, mixed, w_gate, w_up, w_down, w_up.T, w_down.T)


def a2a(x, axis, groups=None):
    return lax.all_to_all(x, axis, 0, 0, tiled=True, axis_index_groups=groups)


def all_reduce_a2a(flat):
    n_ctx = lax.axis_size("ctx")
    n_dp = lax.axis_size("dp")
    rows, width = flat.shape
    core = lax.axis_index("ctx") % 2
    pairs = [(i, i ^ 1) for i in range(n_ctx)]
    groups = [list(range(0, n_ctx, 2)), list(range(1, n_ctx, 2))]
    chips = n_ctx // 2
    half = rows // 2
    part = half // chips
    piece = part // n_dp
    halves = flat.reshape(2, half, width)
    mine = jnp.where(core == 0, halves[0], halves[1])
    other = jnp.where(core == 0, halves[1], halves[0])
    s1 = mine + lax.ppermute(other, "ctx", pairs)
    a = a2a(s1.reshape(chips, part, width), "ctx", groups).sum(0)
    b = a2a(a.reshape(n_dp, piece, width), "dp").sum(0)
    c = a2a(jnp.broadcast_to(b[None], (n_dp, piece, width)), "dp").reshape(part, width)
    d = a2a(jnp.broadcast_to(c[None], (chips, part, width)), "ctx", groups).reshape(half, width)
    e = lax.ppermute(d, "ctx", pairs)
    return jnp.where(core == 0, jnp.concatenate([d, e]), jnp.concatenate([e, d]))


def body(tokens, cotangent, w_gate_value, w_first, w_second, w_up, w_down):
    f32 = jnp.float32
    bf16 = jnp.bfloat16
    n_ctx = lax.axis_size("ctx")
    n_dp = lax.axis_size("dp")
    seq_rows = tokens.shape[1]
    width = tokens.shape[2]
    block_size = w_first.shape[0]
    local_blocks = seq_rows // block_size
    all_blocks = w_second.shape[0]
    per_dev = block_size // n_ctx
    q_n = CHUNKS
    r_n = per_dev // q_n
    seq_in = tokens[0]
    seq_cot = cotangent[0]
    values = jnp.dot(seq_in, w_gate_value[:, width:], preferred_element_type=f32).astype(bf16)
    value_blocks = values.reshape(local_blocks, block_size, width)
    wf = w_first.reshape(block_size, n_ctx, q_n, r_n)
    x5 = seq_in.reshape(local_blocks, n_ctx, q_n, r_n, width)
    c5 = seq_cot.reshape(local_blocks, n_ctx, q_n, r_n, width)

    grad_down = jnp.zeros((w_down.shape[0], width), f32)
    grad_up = jnp.zeros((width, w_up.shape[1]), f32)
    grad_second = jnp.zeros((all_blocks, all_blocks), f32)
    d_values = jnp.zeros((local_blocks, block_size, width), f32)
    outs, d_hiddens, d_gates, gf_parts = [], [], [], []
    for q in range(q_n):
        wf_q = wf[:, :, q, :]
        first_q = jnp.einsum("ijc,jdr->dirc", value_blocks, wf_q, preferred_element_type=f32).astype(bf16)
        first_mid = a2a(first_q, "ctx").reshape(all_blocks, r_n, width)
        mixed_mid = jnp.einsum("ikc,im->mkc", first_mid, w_second, preferred_element_type=f32).astype(bf16)
        mixed = a2a(mixed_mid.reshape(n_ctx, local_blocks, r_n, width), "ctx")
        mixed = mixed.reshape(-1, width)
        xq = x5[:, :, q].transpose(1, 0, 2, 3).reshape(-1, width)
        cq = c5[:, :, q].transpose(1, 0, 2, 3).reshape(-1, width)
        out_q, d_hidden, d_mixed, d_gate, gu, gd = mlp(xq, cq, mixed, w_gate_value[:, :width], w_up, w_down)
        grad_up = grad_up + gu
        grad_down = grad_down + gd
        d_mixed_mid = a2a(d_mixed.reshape(n_ctx, local_blocks, r_n, width), "ctx")
        d_mixed_mid = d_mixed_mid.reshape(all_blocks, r_n, width)
        d_first_mid = jnp.einsum("mkc,im->ikc", d_mixed_mid, w_second, preferred_element_type=f32).astype(bf16)
        grad_second = grad_second + jnp.einsum(
            "ikc,mkc->im", first_mid, d_mixed_mid, preferred_element_type=f32
        )
        d_first = a2a(d_first_mid.reshape(n_ctx, local_blocks, r_n, width), "ctx")
        d_values = d_values + jnp.einsum("dirc,jdr->ijc", d_first, wf_q, preferred_element_type=f32)
        gf_parts.append(jnp.einsum("ijc,dirc->jdr", value_blocks, d_first, preferred_element_type=f32))
        outs.append(out_q.reshape(n_ctx, local_blocks, r_n, width))
        d_hiddens.append(d_hidden.reshape(n_ctx, local_blocks, r_n, width))
        d_gates.append(d_gate.reshape(n_ctx, local_blocks, r_n, width))

    def rows_of(parts):
        return jnp.stack(parts, axis=2).transpose(1, 0, 2, 3, 4).reshape(seq_rows, width)

    output = rows_of(outs)
    d_hidden = rows_of(d_hiddens)
    d_gate = rows_of(d_gates)
    grad_first = jnp.stack(gf_parts, axis=2).reshape(block_size, block_size)
    d_projected = jnp.concatenate([d_gate, d_values.reshape(seq_rows, width)], axis=1).astype(bf16)
    grad_gate_value = jnp.dot(seq_in.T, d_projected, preferred_element_type=f32)
    grad_tokens = (
        d_hidden.astype(f32) + jnp.dot(d_projected, w_gate_value.T, preferred_element_type=f32)
    ).astype(bf16)

    grads = (grad_gate_value, grad_first, grad_second, grad_up, grad_down)
    lane = 128
    flat = jnp.concatenate([g.reshape(-1, lane) for g in grads], axis=0)
    summed = all_reduce_a2a(flat)
    scale = float(seq_rows * n_ctx * n_dp) ** (-0.5)
    summed = summed * scale
    results = []
    at = 0
    for g in grads:
        n = g.size // lane
        results.append(summed[at:at + n].reshape(g.shape))
        at += n
    return (output[None], grad_tokens[None], *results)


def solution(mesh):
    placed = (P("dp", "ctx", None), P("dp", "ctx", None), P(), P(), P(), P(), P())
    return jax.shard_map(
        body,
        mesh=mesh,
        in_specs=placed,
        out_specs=(P("dp", "ctx", None), P("dp", "ctx", None), P(), P(), P(), P(), P()),
        check_vma=False,
    )
```

profile of v0, /device:TPU:1, one launch (start us, length us, event | category | flops | bytes accessed | tf_op | source)
XLA Modules:
  0.0 416.4 jit_solution(3313924558604716565)
XLA Ops:
  10.8 58.7 %all_to_all.40 = bf16[16,32,32,128]{3,2,1,0:T(8,128)(2,1)S(1)} all-to-all(bf16[16,32,32,128]{3,2,1,0:T(8,128)(2,1)S(1)} %copy.51), channel_id=1, replica_groups=mesh['dp'=8,'ctx'=16] {'ctx'}, dimensions={0} | all-to-all | bytes 8388608 | tf_op jit(solution)/shard_map/all_to_all | solution.py:62
  71.5 6.1 %convert_bitcast_fusion.2 = bf16[512,32,128]{0,2,1:T(8,128)(2,1)} fusion(bf16[512,32,128]{2,1,0:T(8,128)(2,1)S(1)} %bitcast.85, bf16[512,512]{1,0:T(8,128)(2,1)S(1)} %copy-done), kind=kOutput, calls=%fused_computation.12 | convolution fusion | flops 2149580800 | bytes 8912896 | tf_op jit(solution)/shard_map/ikc,im->mkc/dot_general | solution.py:118
  77.6 8.0 %copy.53 = bf16[512,32,128]{2,1,0:T(8,128)(2,1)} copy(bf16[512,32,128]{0,2,1:T(8,128)(2,1)} %convert_bitcast_fusion.2) | data formatting | bytes 8388608 | tf_op jit(solution)/shard_map/convert_element_type | solution.py:118
  85.6 5.7 %all-to-all-start.1 = ((bf16[16,32,32,128]{3,2,1,0:T(8,128)(2,1)}), bf16[16,32,32,128]{3,2,1,0:T(8,128)(2,1)}, u32[]{:S(2)}, u32[]{:S(2)}) async-start(bf16[16,32,32,128]{3,2,1,0:T(8,128)(2,1)} %bitcast.88), calls=%async_computation.1 | async-start | bytes 8388608 | tf_op jit(solution)/shard_map/all_to_all | solution.py:62
  93.4 5.5 %copy.49 = bf16[32,16,32,128]{3,2,0,1:T(8,128)(2,1)} copy(bf16[32,16,32,128]{3,2,1,0:T(8,128)(2,1)} %bitcast.96) | data formatting | bytes 8388608 | tf_op jit(solution)/shard_map/squeeze;reshape;squeeze | solution.py:122
  102.0 40.3 %all-to-all-done.1 = bf16[16,32,32,128]{3,2,1,0:T(8,128)(2,1)} async-done(((bf16[16,32,32,128]{3,2,1,0:T(8,128)(2,1)}), bf16[16,32,32,128]{3,2,1,0:T(8,128)(2,1)}, u32[]{:S(2)}, u32[]{:S(2)}) %all-to-all-start.1) | async-done | bytes 4194336 | tf_op jit(solution)/shard_map/all_to_all | solution.py:62
  142.3 26.5 %shard_map.126 = (bf16[16384,128]{1,0:T(8,128)(2,1)}, bf16[16384,128]{1,0:T(8,128)(2,1)}, bf16[16384,128]{1,0:T(8,128)(2,1)}, bf16[16384,128]{1,0:T(8,128)(2,1)}...) custom-call(bf16[16384,128]{1,0:T(8,128)(2,1)} %bitcast.84, bf16[16384,128]{1,0:T(8,128)(2,1)} %bitcast.83, ...), custom_call_target="tpu_custom_call" | custom-call | tf_op jit(solution)/shard_map/pallas_call | solution.py:49
  168.8 55.1 %all_to_all.41 = bf16[16,32,32,128]{3,2,1,0:T(8,128)(2,1)S(1)} all-to-all(bf16[16,32,32,128]{3,2,1,0:T(8,128)(2,1)} %bitcast.106), channel_id=1, replica_groups=mesh['dp'=8,'ctx'=16] {'ctx'}, dimensions={0} | all-to-all | bytes 8388608 | tf_op jit(solution)/shard_map/all_to_all | solution.py:62
  225.9 6.4 %convert_bitcast_fusion.1 = bf16[512,32,128]{0,2,1:T(8,128)(2,1)} fusion(bf16[512,32,128]{2,1,0:T(8,128)(2,1)S(1)} %bitcast.104, bf16[512,512]{1,0:T(8,128)(2,1)S(1)} %copy-done), kind=kOutput, calls=%fused_computation.11 | convolution fusion | flops 2149580800 | bytes 8912896 | tf_op jit(solution)/shard_map/mkc,im->ikc/dot_general | solution.py:128
  232.2 7.8 %copy.60 = bf16[512,32,128]{2,1,0:T(8,128)(2,1)} copy(bf16[512,32,128]{0,2,1:T(8,128)(2,1)} %convert_bitcast_fusion.1) | data formatting | bytes 8388608 | tf_op jit(solution)/shard_map/convert_element_type | solution.py:128
  240.1 5.7 %all-to-all-start.3 = ((bf16[16,32,32,128]{3,2,1,0:T(8,128)(2,1)}), bf16[16,32,32,128]{3,2,1,0:T(8,128)(2,1)}, u32[]{:S(2)}, u32[]{:S(2)}) async-start(bf16[16,32,32,128]{3,2,1,0:T(8,128)(2,1)} %bitcast.87), calls=%async_computation.3 | async-start | bytes 8388608 | tf_op jit(solution)/shard_map/all_to_all | solution.py:62
  245.8 5.6 %copy.58 = bf16[16,32,1,32,128]{4,3,0,1,2:T(8,128)(2,1)} copy(bf16[16,32,1,32,128]{4,3,1,0,2:T(8,128)(2,1)} %bitcast.102) | data formatting | bytes 8388608 | tf_op jit(solution)/shard_map/convert_element_type | solution.py:146
  256.1 40.7 %all-to-all-done.3 = bf16[16,32,32,128]{3,2,1,0:T(8,128)(2,1)} async-done(((bf16[16,32,32,128]{3,2,1,0:T(8,128)(2,1)}), bf16[16,32,32,128]{3,2,1,0:T(8,128)(2,1)}, u32[]{:S(2)}, u32[]{:S(2)}) %all-to-all-start.3) | async-done | bytes 4194336 | tf_op jit(solution)/shard_map/all_to_all | solution.py:62
  296.8 6.6 %fusion.3 = bf16[32,512,128]{1,2,0:T(8,128)(2,1)} fusion(bf16[16,32,32,128]{3,2,1,0:T(8,128)(2,1)} %all-to-all-done.3, bf16[512,16,32,1]{0,2,3,1:T(8,128)(2,1)S(1)} %bitcast.108), kind=kOutput, calls=%fused_computation.8 | convolution fusion | flops 2149580800 | bytes 8912896 | tf_op jit(solution)/shard_map/dirc,jdr->ijc/dot_general | solution.py:133
  303.3 6.5 %copy.62 = bf16[32,512,128]{2,1,0:T(8,128)(2,1)} copy(bf16[32,512,128]{1,2,0:T(8,128)(2,1)} %fusion.3) | data formatting | bytes 8388608 | tf_op jit(solution)/shard_map/dirc,jdr->ijc/transpose | solution.py:133
  309.8 5.8 %convolution_bitcast_fusion = f32[512,16,32]{0,2,1:T(8,128)S(1)} fusion(bf16[32,512,128,1]{2,1,0,3:T(8,128)(2,1)} %bitcast.91, bf16[16,32,32,128]{3,2,1,0:T(8,128)(2,1)} %all-to-all-done.3), kind=kOutput, calls=%fused_computation.24 | convolution fusion | flops 2147483648 | bytes 9437184 | tf_op jit(solution)/shard_map/ijc,dirc->jdr/dot_general | solution.py:134
  322.6 7.1 %fusion.23 = f32[128,256]{0,1:T(8,128)S(1)} fusion(bf16[1,16384,128]{2,1,0:T(8,128)(2,1)} %param.7, bf16[16384,128]{1,0:T(8,128)(2,1)} %bitcast.100, bf16[16384,128]{1,0:T(8,128)(2,1)} %bitcast.98), kind=kOutput, calls=%fused_computation.30 | convolution fusion | flops 1090519040 | bytes 12713984 | tf_op jit(solution)/shard_map/dot_general | solution.py:147
  333.8 21.3 %all_to_all.42 = f32[8,304,128]{2,1,0:T(8,128)S(1)} all-to-all(f32[8,304,128]{2,1,0:T(8,128)S(1)} %bitcast.94), channel_id=1, replica_groups={{0,2,4,6,8,10,12,14},{1,3,5,7,9,11,13,15},{16,18,20,22,24,26,28,30},{17..., dimensions={0} | all-to-all | bytes 2490368 | tf_op jit(solution)/shard_map/all_to_all | solution.py:62
  355.2 10.5 %all_to_all.43 = f32[8,38,128]{2,1,0:T(8,128)S(1)} all-to-all(f32[8,38,128]{2,1,0:T(8,128)S(1)} %reshape.106), channel_id=1, replica_groups=mesh['dp'=8,'ctx'=16] {'dp'}, dimensions={0} | all-to-all | bytes 311296 | tf_op jit(solution)/shard_map/all_to_all | solution.py:62
  365.7 8.2 %all_to_all.44 = f32[8,38,128]{2,1,0:T(8,128)S(1)} all-to-all(f32[8,38,128]{2,1,0:T(8,128)S(1)} %broadcast_in_dim.17), channel_id=1, replica_groups=mesh['dp'=8,'ctx'=16] {'dp'}, dimensions={0} | all-to-all | bytes 311296 | tf_op jit(solution)/shard_map/all_to_all | solution.py:62
  378.6 5.5 %copy.56 = bf16[32,16,1,32,128]{4,3,1,0,2:T(8,128)(2,1)} copy(bf16[32,16,1,32,128]{4,3,0,1,2:T(8,128)(2,1)} %bitcast.97) | data formatting | bytes 8388608 | tf_op jit(solution)/shard_map/transpose | solution.py:140
  384.1 9.8 %all-to-all-done.7 = f32[8,304,128]{2,1,0:T(8,128)S(1)} async-done(((f32[8,304,128]{2,1,0:T(8,128)}), f32[8,304,128]{2,1,0:T(8,128)S(1)}, u32[]{:S(2)}, u32[]{:S(2)}) %all-to-all-start.7) | async-done | bytes 1245216 | tf_op jit(solution)/shard_map/all_to_all | solution.py:62
  393.8 5.0 %collective-permute-start.1 = (f32[2432,128]{1,0:T(8,128)S(1)}, f32[2432,128]{1,0:T(8,128)S(1)}, u32[]{:S(2)}, u32[]{:S(2)}) collective-permute-start(f32[2432,128]{1,0:T(8,128)S(1)} %bitcast.92), channel_id=1, source_target_pairs={{0,1},{1,0},{2,3},{3,2},{4,5},{5,4},{6,7},{7,6},{8,9},{9,8},{10,11... | collective-permute-start | bytes 3735560 | tf_op jit(solution)/shard_map/ppermute | solution.py:84
  403.6 7.9 %fusion.1 = bf16[1,16384,128]{2,1,0:T(8,128)(2,1)} fusion(f32[16384,128]{1,0:T(8,128)S(1)} %bitcast.89, bf16[128,256]{1,0:T(8,128)(2,1)S(1)} %copy-done.12, bf16[16384,128]{1,0:T(8,128)(2,1)} %bitcast.101, bf16[16384,128]{1,0:T(8,128)(2,1)} %bitcast.99), kind=kOutput, calls=%fused_computation.3 | convolution fusion | flops 1094713344 | bytes 21037056 | tf_op jit(solution)/shard_map/dot_general | solution.py:149
  (62 shorter events, 49.5 us)
Async XLA Ops:
  0.6 70.9 %copy-start = (bf16[512,512]{1,0:T(8,128)(2,1)S(1)}, bf16[512,512]{1,0:T(8,128)(2,1)}, u32[]{:S(2)}) copy-start(bf16[512,512]{1,0:T(8,128)(2,1)} %param.11) | copy-start | bytes 1572868
  5.4 2.0 copy-start.5
  69.6 2.0 copy-start.3
  85.6 5.7 %copy-start.12 = (bf16[128,256]{1,0:T(8,128)(2,1)S(1)}, bf16[128,256]{1,0:T(8,128)(2,1)}, u32[]{:S(2)}) copy-start(bf16[128,256]{1,0:T(8,128)(2,1)} %param.9) | copy-start | bytes 196612
  85.6 6.3 %copy-start.9 = (bf16[128,256]{1,0:T(8,128)(2,1)S(1)}, bf16[128,256]{1,0:T(8,128)(2,1)}, u32[]{:S(2)}) copy-start(bf16[128,256]{1,0:T(8,128)(2,1)} %wu_ref.1) | copy-start | bytes 196612
  85.6 7.0 %copy-start.10 = (bf16[256,128]{1,0:T(8,128)(2,1)S(1)}, bf16[256,128]{1,0:T(8,128)(2,1)}, u32[]{:S(2)}) copy-start(bf16[256,128]{1,0:T(8,128)(2,1)} %wd_ref.1) | copy-start | bytes 196612
  85.6 56.7 %all-to-all-start.1 = ((bf16[16,32,32,128]{3,2,1,0:T(8,128)(2,1)}), bf16[16,32,32,128]{3,2,1,0:T(8,128)(2,1)}, u32[]{:S(2)}, u32[]{:S(2)}) async-start(bf16[16,32,32,128]{3,2,1,0:T(8,128)(2,1)} %bitcast.88), calls=%async_computation.1 | async-start | bytes 8388608 | tf_op jit(solution)/shard_map/all_to_all | solution.py:62
  93.4 5.5 %copy-start.2 = (bf16[1,16384,128]{2,1,0:T(8,128)(2,1)S(1)}, bf16[1,16384,128]{2,1,0:T(8,128)(2,1)}, u32[]{:S(2)}) copy-start(bf16[1,16384,128]{2,1,0:T(8,128)(2,1)} %param.7) | copy-start | bytes 12582916
  223.9 1.9 copy-start.6
  240.1 5.7 %copy-start.11 = (f32[128,256]{1,0:T(8,128)S(1)}, f32[128,256]{1,0:T(8,128)}, u32[]{:S(2)}) copy-start(f32[128,256]{1,0:T(8,128)} %get-tuple-element.17) | copy-start | bytes 393220
  240.1 56.7 %all-to-all-start.3 = ((bf16[16,32,32,128]{3,2,1,0:T(8,128)(2,1)}), bf16[16,32,32,128]{3,2,1,0:T(8,128)(2,1)}, u32[]{:S(2)}, u32[]{:S(2)}) async-start(bf16[16,32,32,128]{3,2,1,0:T(8,128)(2,1)} %bitcast.87), calls=%async_computation.3 | async-start | bytes 8388608 | tf_op jit(solution)/shard_map/all_to_all | solution.py:62
  245.8 5.6 %copy-start.4 = (bf16[16,32,32,128]{3,2,1,0:T(8,128)(2,1)S(1)}, bf16[16,32,32,128]{3,2,1,0:T(8,128)(2,1)}, u32[]{:S(2)}) copy-start(bf16[16,32,32,128]{3,2,1,0:T(8,128)(2,1)} %copy-done.3) | copy-start | bytes 12582916
  245.8 5.6 %copy-start.7 = (bf16[16,32,32,128]{3,2,1,0:T(8,128)(2,1)S(1)}, bf16[16,32,32,128]{3,2,1,0:T(8,128)(2,1)}, u32[]{:S(2)}) copy-start(bf16[16,32,32,128]{3,2,1,0:T(8,128)(2,1)} %copy-done.6) | copy-start | bytes 12582916
  322.6 7.2 %copy-start.8 = (f32[256,128]{1,0:T(8,128)S(1)}, f32[256,128]{1,0:T(8,128)}, u32[]{:S(2)}) copy-start(f32[256,128]{1,0:T(8,128)} %get-tuple-element.18) | copy-start | bytes 393220
  330.0 3.7 collective-permute-start
  375.0 18.8 %all-to-all-start.7 = ((f32[8,304,128]{2,1,0:T(8,128)}), f32[8,304,128]{2,1,0:T(8,128)S(1)}, u32[]{:S(2)}, u32[]{:S(2)}) async-start(f32[8,304,128]{2,1,0:T(8,128)} %broadcast_in_dim.19), calls=%async_computation.7 | async-start | bytes 2490368 | tf_op jit(solution)/shard_map/all_to_all | solution.py:62
  393.8 17.7 %collective-permute-start.1 = (f32[2432,128]{1,0:T(8,128)S(1)}, f32[2432,128]{1,0:T(8,128)S(1)}, u32[]{:S(2)}, u32[]{:S(2)}) collective-permute-start(f32[2432,128]{1,0:T(8,128)S(1)} %bitcast.92), channel_id=1, source_target_pairs={{0,1},{1,0},{2,3},{3,2},{4,5},{5,4},{6,7},{7,6},{8,9},{9,8},{10,11... | collective-permute-start | bytes 3735560 | tf_op jit(solution)/shard_map/ppermute | solution.py:84
  411.9 4.5 %copy-start.1 = (bf16[512,512]{1,0:T(8,128)(2,1)S(1)}, bf16[512,512]{1,0:T(8,128)(2,1)}, u32[]{:S(2)}) copy-start(bf16[512,512]{1,0:T(8,128)(2,1)} %param.11) | copy-start | bytes 1572868
where the time goes:
time: 418 us; the launch traced here: 416 us
  blocking collectives  154 us (37%)
  waiting for transfers between devices  93.4 us (22%)
  local copies, waits for them, and re-layouts  67.7 us (16%)
  matrix products  49 us (12%)
  Pallas kernels  26.5 us (6%)
  starting transfers between devices  21 us (5%)
    all_to_all x5, blocking collectives, a2a(): return lax.all_to_all(x, axis, 0, 0, tiled=True, axis_index_groups=groups)  154 us
    all_to_all x3, waiting for transfers between devices, a2a(): return lax.all_to_all(x, axis, 0, 0, tiled=True, axis_index_groups=groups)  90.8 us
    pallas_call x1, Pallas kernels, mlp(): pl.pallas_call(mlp_kernel, grid=(rows // tile,), in_specs=[row, row, row,...  26.5 us
    all_to_all x3, starting transfers between devices, a2a(): return lax.all_to_all(x, axis, 0, 0, tiled=True, axis_index_groups=groups)  14.9 us
    unnamed x29, local copies, waits for them, and re-layouts  8.72 us
  transfers between devices with their start and end apart: 5, of which 4 were waited for; matrix products, arithmetic and copies ran while one was open for 9% of the time, Pallas kernels for 0%

commit v1 on v0

--- a/solution.py
+++ b/solution.py
@@ -58,6 +58,23 @@
     )(x, cot, mixed, w_gate, w_up, w_down, w_up.T, w_down.T)
 
 
+def mix_kernel(a_ref, f_ref, o_ref):
+    a = a_ref[...]
+    for kk in range(f_ref.shape[1]):
+        o_ref[:, kk, :] = jnp.dot(a, f_ref[:, kk, :], preferred_element_type=jnp.float32).astype(o_ref.dtype)
+
+def mix(a, f, kb=16):
+    n, k, c = f.shape
+    blk = pl.BlockSpec((n, kb, c), lambda i: (0, i, 0))
+    return pl.pallas_call(
+        mix_kernel,
+        grid=(k // kb,),
+        in_specs=[pl.BlockSpec(a.shape, lambda i: (0, 0)), blk],
+        out_specs=blk,
+        out_shape=jax.ShapeDtypeStruct(f.shape, jnp.bfloat16),
+    )(a, f)
+
+
 def a2a(x, axis, groups=None):
     return lax.all_to_all(x, axis, 0, 0, tiled=True, axis_index_groups=groups)
 
@@ -115,7 +132,7 @@
         wf_q = wf[:, :, q, :]
         first_q = jnp.einsum("ijc,jdr->dirc", value_blocks, wf_q, preferred_element_type=f32).astype(bf16)
         first_mid = a2a(first_q, "ctx").reshape(all_blocks, r_n, width)
-        mixed_mid = jnp.einsum("ikc,im->mkc", first_mid, w_second, preferred_element_type=f32).astype(bf16)
+        mixed_mid = mix(w_second.T, first_mid)
         mixed = a2a(mixed_mid.reshape(n_ctx, local_blocks, r_n, width), "ctx")
         mixed = mixed.reshape(-1, width)
         xq = x5[:, :, q].transpose(1, 0, 2, 3).reshape(-1, width)
@@ -125,7 +142,7 @@
         grad_down = grad_down + gd
         d_mixed_mid = a2a(d_mixed.reshape(n_ctx, local_blocks, r_n, width), "ctx")
         d_mixed_mid = d_mixed_mid.reshape(all_blocks, r_n, width)
-        d_first_mid = jnp.einsum("mkc,im->ikc", d_mixed_mid, w_second, preferred_element_type=f32).astype(bf16)
+        d_first_mid = mix(w_second, d_mixed_mid)
         grad_second = grad_second + jnp.einsum(
             "ikc,mkc->im", first_mid, d_mixed_mid, preferred_element_type=f32
         )

time: 418 us -> 434 us (1.038)
  blocking collectives: 154 us -> 96.3 us
  waiting for transfers between devices: 93.4 us -> 143 us
  Pallas kernels: 26.5 us -> 67.1 us
  local copies, waits for them, and re-layouts: 67.7 us -> 49.7 us
  matrix products: 49 us -> 37.8 us
  starting transfers between devices: 21 us -> 30.2 us
    all_to_all x5 -> x4, blocking collectives: 154 us -> 96.3 us  [a2a(): return lax.all_to_all(x, axis, 0, 0, tiled=True, axis_index_groups=groups)]
    all_to_all x3 -> x4, waiting for transfers between devices: 90.8 us -> 140 us  [a2a(): return lax.all_to_all(x, axis, 0, 0, tiled=True, axis_index_groups=groups)]
    pallas_call x0 -> x2, Pallas kernels: none -> 40.6 us  [mix(): pl.pallas_call(mix_kernel, grid=(k // kb,), in_specs=[pl.BlockSpec(a.shap...]
    convert_element_type x2 -> x0, local copies, waits for them, and re-layouts: 15.8 us -> none  [the longest x1 7.99 us: body(): jnp.einsum('ikc,im->mkc', first_mid, w_second, preferred_element_type=f32)]
    dot_general x2 -> x0, matrix products: 12.4 us -> none  [the longest x1 6.36 us: body(): jnp.einsum('mkc,im->ikc', d_mixed_mid, w_second, preferred_element_type=f32)]
    all_to_all x3 -> x4, starting transfers between devices: 14.9 us -> 24.1 us  [a2a(): return lax.all_to_all(x, axis, 0, 0, tiled=True, axis_index_groups=groups)]
    unnamed x29 -> x22, local copies, waits for them, and re-layouts: 8.72 us -> 5.73 us
  transfers between devices with their start and end apart: 5 -> 6, of which waited for: 4 -> 5; matrix products, arithmetic and copies ran while one was open for 9% -> 9% of each run, Pallas kernels for 0% -> 0%
where the time goes in v1:
time: 434 us; the launch traced here: 429 us
  waiting for transfers between devices  143 us (33%)
  blocking collectives  96.3 us (22%)
  Pallas kernels  67.1 us (15%)
  local copies, waits for them, and re-layouts  49.7 us (11%)
  matrix products  37.8 us (9%)
  starting transfers between devices  30.2 us (7%)
    all_to_all x4, waiting for transfers between devices, a2a(): return lax.all_to_all(x, axis, 0, 0, tiled=True, axis_index_groups=groups)  140 us
    all_to_all x4, blocking collectives, a2a(): return lax.all_to_all(x, axis, 0, 0, tiled=True, axis_index_groups=groups)  96.3 us
    pallas_call x2, Pallas kernels, mix(): pl.pallas_call(mix_kernel, grid=(k // kb,), in_specs=[pl.BlockSpec(a.shap...  40.6 us
    pallas_call x1, Pallas kernels, mlp(): pl.pallas_call(mlp_kernel, grid=(rows // tile,), in_specs=[row, row, row,...  26.5 us
    all_to_all x4, starting transfers between devices, a2a(): return lax.all_to_all(x, axis, 0, 0, tiled=True, axis_index_groups=groups)  24.1 us
  transfers between devices with their start and end apart: 6, of which 5 were waited for; matrix products, arithmetic and copies ran while one was open for 9% of the time, Pallas kernels for 0%

profile of v1, /device:TPU:1, one launch (start us, length us, event | category | flops | bytes accessed | tf_op | source)
XLA Modules:
  0.0 429.3 jit_solution(3187911555228002186)
XLA Ops:
  12.8 8.9 %all-to-all-start = ((bf16[16,32,32,128]{3,2,1,0:T(8,128)(2,1)}), bf16[16,32,32,128]{3,2,1,0:T(8,128)(2,1)}, u32[]{:S(2)}, u32[]{:S(2)}) async-start(bf16[16,32,32,128]{3,2,1,0:T(8,128)(2,1)} %copy.49), calls=%async_computation | async-start | bytes 8388608 | tf_op jit(solution)/shard_map/all_to_all | solution.py:79
  22.7 49.7 %all-to-all-done = bf16[16,32,32,128]{3,2,1,0:T(8,128)(2,1)} async-done(((bf16[16,32,32,128]{3,2,1,0:T(8,128)(2,1)}), bf16[16,32,32,128]{3,2,1,0:T(8,128)(2,1)}, u32[]{:S(2)}, u32[]{:S(2)}) %all-to-all-start) | async-done | bytes 4194336 | tf_op jit(solution)/shard_map/all_to_all | solution.py:79
  72.4 20.3 %shard_map.126 = bf16[512,32,128]{2,1,0:T(8,128)(2,1)} custom-call(bf16[512,512]{1,0:T(8,128)(2,1)} %bitcast.99, bf16[512,32,128]{2,1,0:T(8,128)(2,1)} %bitcast.14.f_ref), custom_call_target="tpu_custom_call" | custom-call | tf_op jit(solution)/shard_map/pallas_call | solution.py:69
  92.8 5.4 %all-to-all-start.1 = ((bf16[16,32,32,128]{3,2,1,0:T(8,128)(2,1)}), bf16[16,32,32,128]{3,2,1,0:T(8,128)(2,1)}, u32[]{:S(2)}, u32[]{:S(2)}) async-start(bf16[16,32,32,128]{3,2,1,0:T(8,128)(2,1)} %bitcast.80), calls=%async_computation.1 | async-start | bytes 8388608 | tf_op jit(solution)/shard_map/all_to_all | solution.py:79
  100.3 5.5 %copy.46 = bf16[32,16,32,128]{3,2,0,1:T(8,128)(2,1)} copy(bf16[32,16,32,128]{3,2,1,0:T(8,128)(2,1)} %bitcast.88) | data formatting | bytes 8388608 | tf_op jit(solution)/shard_map/squeeze;reshape;squeeze | solution.py:139
  108.9 40.3 %all-to-all-done.1 = bf16[16,32,32,128]{3,2,1,0:T(8,128)(2,1)} async-done(((bf16[16,32,32,128]{3,2,1,0:T(8,128)(2,1)}), bf16[16,32,32,128]{3,2,1,0:T(8,128)(2,1)}, u32[]{:S(2)}, u32[]{:S(2)}) %all-to-all-start.1) | async-done | bytes 4194336 | tf_op jit(solution)/shard_map/all_to_all | solution.py:79
  149.2 26.5 %shard_map.127 = (bf16[16384,128]{1,0:T(8,128)(2,1)}, bf16[16384,128]{1,0:T(8,128)(2,1)}, bf16[16384,128]{1,0:T(8,128)(2,1)}, bf16[16384,128]{1,0:T(8,128)(2,1)}...) custom-call(bf16[16384,128]{1,0:T(8,128)(2,1)} %bitcast.76, bf16[16384,128]{1,0:T(8,128)(2,1)} %bitcast.75, ...), custom_call_target="tpu_custom_call" | custom-call | tf_op jit(solution)/shard_map/pallas_call | solution.py:49
  175.7 56.2 %all_to_all.40 = bf16[16,32,32,128]{3,2,1,0:T(8,128)(2,1)} all-to-all(bf16[16,32,32,128]{3,2,1,0:T(8,128)(2,1)} %bitcast.96), channel_id=1, replica_groups=mesh['dp'=8,'ctx'=16] {'ctx'}, dimensions={0} | all-to-all | bytes 8388608 | tf_op jit(solution)/shard_map/all_to_all | solution.py:79
  231.9 20.3 %shard_map.128 = bf16[512,32,128]{2,1,0:T(8,128)(2,1)} custom-call(bf16[512,512]{1,0:T(8,128)(2,1)} %a_ref.1, bf16[512,32,128]{2,1,0:T(8,128)(2,1)} %bitcast.78), custom_call_target="tpu_custom_call" | custom-call | tf_op jit(solution)/shard_map/pallas_call | solution.py:69
  252.2 6.2 %all-to-all-start.3 = ((bf16[16,32,32,128]{3,2,1,0:T(8,128)(2,1)}), bf16[16,32,32,128]{3,2,1,0:T(8,128)(2,1)}, u32[]{:S(2)}, u32[]{:S(2)}) async-start(bf16[16,32,32,128]{3,2,1,0:T(8,128)(2,1)} %bitcast.77), calls=%async_computation.3 | async-start | bytes 8388608 | tf_op jit(solution)/shard_map/all_to_all | solution.py:79
  258.5 5.6 %copy.54 = bf16[16,32,1,32,128]{4,3,0,1,2:T(8,128)(2,1)} copy(bf16[16,32,1,32,128]{4,3,1,0,2:T(8,128)(2,1)} %bitcast.94) | data formatting | bytes 8388608 | tf_op jit(solution)/shard_map/convert_element_type | solution.py:163
  264.0 4.6 %fusion.10 = f32[512,512]{1,0:T(8,128)S(1)} fusion(bf16[512,32,128]{2,1,0:T(8,128)(2,1)S(1)} %bitcast.79, bf16[512,32,128]{2,1,0:T(8,128)(2,1)} %bitcast.14.f_ref), kind=kOutput, calls=%fused_computation.17 | convolution fusion | flops 2147483648 | bytes 9437184 | tf_op jit(solution)/shard_map/ikc,mkc->im/dot_general | solution.py:146
  268.7 40.5 %all-to-all-done.3 = bf16[16,32,32,128]{3,2,1,0:T(8,128)(2,1)} async-done(((bf16[16,32,32,128]{3,2,1,0:T(8,128)(2,1)}), bf16[16,32,32,128]{3,2,1,0:T(8,128)(2,1)}, u32[]{:S(2)}, u32[]{:S(2)}) %all-to-all-start.3) | async-done | bytes 4194336 | tf_op jit(solution)/shard_map/all_to_all | solution.py:79
  309.3 6.6 %fusion.3 = bf16[32,512,128]{1,2,0:T(8,128)(2,1)} fusion(bf16[16,32,32,128]{3,2,1,0:T(8,128)(2,1)} %all-to-all-done.3, bf16[512,16,32,1]{0,2,3,1:T(8,128)(2,1)S(1)} %bitcast.98), kind=kOutput, calls=%fused_computation.8 | convolution fusion | flops 2149580800 | bytes 8912896 | tf_op jit(solution)/shard_map/dirc,jdr->ijc/dot_general | solution.py:150
  315.8 6.5 %copy.56 = bf16[32,512,128]{2,1,0:T(8,128)(2,1)} copy(bf16[32,512,128]{1,2,0:T(8,128)(2,1)} %fusion.3) | data formatting | bytes 8388608 | tf_op jit(solution)/shard_map/dirc,jdr->ijc/transpose | solution.py:150
  322.3 5.8 %convolution_bitcast_fusion = f32[512,16,32]{0,2,1:T(8,128)S(1)} fusion(bf16[32,512,128,1]{2,1,0,3:T(8,128)(2,1)} %bitcast.83, bf16[16,32,32,128]{3,2,1,0:T(8,128)(2,1)} %all-to-all-done.3), kind=kOutput, calls=%fused_computation.18 | convolution fusion | flops 2147483648 | bytes 9437184 | tf_op jit(solution)/shard_map/ijc,dirc->jdr/dot_general | solution.py:151
  335.1 7.1 %fusion.15 = f32[128,256]{0,1:T(8,128)S(1)} fusion(bf16[1,16384,128]{2,1,0:T(8,128)(2,1)} %param.7, bf16[16384,128]{1,0:T(8,128)(2,1)} %bitcast.92, bf16[16384,128]{1,0:T(8,128)(2,1)} %bitcast.90), kind=kOutput, calls=%fused_computation.24 | convolution fusion | flops 1090519040 | bytes 12713984 | tf_op jit(solution)/shard_map/dot_general | solution.py:164
  346.3 21.3 %all_to_all.41 = f32[8,304,128]{2,1,0:T(8,128)S(1)} all-to-all(f32[8,304,128]{2,1,0:T(8,128)S(1)} %bitcast.86), channel_id=1, replica_groups={{0,2,4,6,8,10,12,14},{1,3,5,7,9,11,13,15},{16,18,20,22,24,26,28,30},{17..., dimensions={0} | all-to-all | bytes 2490368 | tf_op jit(solution)/shard_map/all_to_all | solution.py:79
  367.7 10.5 %all_to_all.42 = f32[8,38,128]{2,1,0:T(8,128)S(1)} all-to-all(f32[8,38,128]{2,1,0:T(8,128)S(1)} %reshape.106), channel_id=1, replica_groups=mesh['dp'=8,'ctx'=16] {'dp'}, dimensions={0} | all-to-all | bytes 311296 | tf_op jit(solution)/shard_map/all_to_all | solution.py:79
  378.3 8.3 %all_to_all.43 = f32[8,38,128]{2,1,0:T(8,128)S(1)} all-to-all(f32[8,38,128]{2,1,0:T(8,128)S(1)} %broadcast_in_dim.17), channel_id=1, replica_groups=mesh['dp'=8,'ctx'=16] {'dp'}, dimensions={0} | all-to-all | bytes 311296 | tf_op jit(solution)/shard_map/all_to_all | solution.py:79
  391.3 5.5 %copy.52 = bf16[32,16,1,32,128]{4,3,1,0,2:T(8,128)(2,1)} copy(bf16[32,16,1,32,128]{4,3,0,1,2:T(8,128)(2,1)} %bitcast.89) | data formatting | bytes 8388608 | tf_op jit(solution)/shard_map/transpose | solution.py:157
  396.8 9.8 %all-to-all-done.7 = f32[8,304,128]{2,1,0:T(8,128)S(1)} async-done(((f32[8,304,128]{2,1,0:T(8,128)}), f32[8,304,128]{2,1,0:T(8,128)S(1)}, u32[]{:S(2)}, u32[]{:S(2)}) %all-to-all-start.7) | async-done | bytes 1245216 | tf_op jit(solution)/shard_map/all_to_all | solution.py:79
  406.5 5.0 %collective-permute-start.1 = (f32[2432,128]{1,0:T(8,128)S(1)}, f32[2432,128]{1,0:T(8,128)S(1)}, u32[]{:S(2)}, u32[]{:S(2)}) collective-permute-start(f32[2432,128]{1,0:T(8,128)S(1)} %bitcast.84), channel_id=1, source_target_pairs={{0,1},{1,0},{2,3},{3,2},{4,5},{5,4},{6,7},{7,6},{8,9},{9,8},{10,11... | collective-permute-start | bytes 3735560 | tf_op jit(solution)/shard_map/ppermute | solution.py:101
  416.3 7.9 %fusion.1 = bf16[1,16384,128]{2,1,0:T(8,128)(2,1)} fusion(f32[16384,128]{1,0:T(8,128)S(1)} %bitcast.81, bf16[128,256]{1,0:T(8,128)(2,1)S(1)} %copy-done.8, bf16[16384,128]{1,0:T(8,128)(2,1)} %bitcast.93, bf16[16384,128]{1,0:T(8,128)(2,1)} %bitcast.91), kind=kOutput, calls=%fused_computation.3 | convolution fusion | flops 1094713344 | bytes 21037056 | tf_op jit(solution)/shard_map/dot_general | solution.py:166
  (54 shorter events, 43.9 us)
Async XLA Ops:
  5.3 2.0 copy-start.2
  12.8 8.9 %copy-start.3 = (bf16[512,512]{1,0:T(8,128)(2,1)S(1)}, bf16[512,512]{1,0:T(8,128)(2,1)}, u32[]{:S(2)}) copy-start(bf16[512,512]{1,0:T(8,128)(2,1)} %a_ref.1) | copy-start | bytes 1572868
  12.8 59.6 %all-to-all-start = ((bf16[16,32,32,128]{3,2,1,0:T(8,128)(2,1)}), bf16[16,32,32,128]{3,2,1,0:T(8,128)(2,1)}, u32[]{:S(2)}, u32[]{:S(2)}) async-start(bf16[16,32,32,128]{3,2,1,0:T(8,128)(2,1)} %copy.49), calls=%async_computation | async-start | bytes 8388608 | tf_op jit(solution)/shard_map/all_to_all | solution.py:79
  92.7 5.4 %copy-start.8 = (bf16[128,256]{1,0:T(8,128)(2,1)S(1)}, bf16[128,256]{1,0:T(8,128)(2,1)}, u32[]{:S(2)}) copy-start(bf16[128,256]{1,0:T(8,128)(2,1)} %param.9) | copy-start | bytes 196612
  92.7 6.1 %copy-start.5 = (bf16[128,256]{1,0:T(8,128)(2,1)S(1)}, bf16[128,256]{1,0:T(8,128)(2,1)}, u32[]{:S(2)}) copy-start(bf16[128,256]{1,0:T(8,128)(2,1)} %wu_ref.1) | copy-start | bytes 196612
  92.8 6.8 %copy-start.6 = (bf16[256,128]{1,0:T(8,128)(2,1)S(1)}, bf16[256,128]{1,0:T(8,128)(2,1)}, u32[]{:S(2)}) copy-start(bf16[256,128]{1,0:T(8,128)(2,1)} %wd_ref.1) | copy-start | bytes 196612
  92.8 56.4 %all-to-all-start.1 = ((bf16[16,32,32,128]{3,2,1,0:T(8,128)(2,1)}), bf16[16,32,32,128]{3,2,1,0:T(8,128)(2,1)}, u32[]{:S(2)}, u32[]{:S(2)}) async-start(bf16[16,32,32,128]{3,2,1,0:T(8,128)(2,1)} %bitcast.80), calls=%async_computation.1 | async-start | bytes 8388608 | tf_op jit(solution)/shard_map/all_to_all | solution.py:79
  100.3 5.5 %copy-start = (bf16[1,16384,128]{2,1,0:T(8,128)(2,1)S(1)}, bf16[1,16384,128]{2,1,0:T(8,128)(2,1)}, u32[]{:S(2)}) copy-start(bf16[1,16384,128]{2,1,0:T(8,128)(2,1)} %param.7) | copy-start | bytes 12582916
  252.2 6.2 %copy-start.7 = (f32[128,256]{1,0:T(8,128)S(1)}, f32[128,256]{1,0:T(8,128)}, u32[]{:S(2)}) copy-start(f32[128,256]{1,0:T(8,128)} %get-tuple-element.17) | copy-start | bytes 393220
  252.2 57.1 %all-to-all-start.3 = ((bf16[16,32,32,128]{3,2,1,0:T(8,128)(2,1)}), bf16[16,32,32,128]{3,2,1,0:T(8,128)(2,1)}, u32[]{:S(2)}, u32[]{:S(2)}) async-start(bf16[16,32,32,128]{3,2,1,0:T(8,128)(2,1)} %bitcast.77), calls=%async_computation.3 | async-start | bytes 8388608 | tf_op jit(solution)/shard_map/all_to_all | solution.py:79
  258.5 5.6 %copy-start.1 = (bf16[16,32,32,128]{3,2,1,0:T(8,128)(2,1)S(1)}, bf16[16,32,32,128]{3,2,1,0:T(8,128)(2,1)}, u32[]{:S(2)}) copy-start(bf16[16,32,32,128]{3,2,1,0:T(8,128)(2,1)} %all_to_all.40) | copy-start | bytes 12582916
  335.1 7.2 %copy-start.4 = (f32[256,128]{1,0:T(8,128)S(1)}, f32[256,128]{1,0:T(8,128)}, u32[]{:S(2)}) copy-start(f32[256,128]{1,0:T(8,128)} %get-tuple-element.18) | copy-start | bytes 393220
  342.5 3.7 collective-permute-start
  387.7 18.8 %all-to-all-start.7 = ((f32[8,304,128]{2,1,0:T(8,128)}), f32[8,304,128]{2,1,0:T(8,128)S(1)}, u32[]{:S(2)}, u32[]{:S(2)}) async-start(f32[8,304,128]{2,1,0:T(8,128)} %broadcast_in_dim.19), calls=%async_computation.7 | async-start | bytes 2490368 | tf_op jit(solution)/shard_map/all_to_all | solution.py:79
  406.5 17.7 %collective-permute-start.1 = (f32[2432,128]{1,0:T(8,128)S(1)}, f32[2432,128]{1,0:T(8,128)S(1)}, u32[]{:S(2)}, u32[]{:S(2)}) collective-permute-start(f32[2432,128]{1,0:T(8,128)S(1)} %bitcast.84), channel_id=1, source_target_pairs={{0,1},{1,0},{2,3},{3,2},{4,5},{5,4},{6,7},{7,6},{8,9},{9,8},{10,11... | collective-permute-start | bytes 3735560 | tf_op jit(solution)/shard_map/ppermute | solution.py:101

commit v2 on v0

--- a/solution.py
+++ b/solution.py
@@ -72,14 +72,16 @@
     chips = n_ctx // 2
     half = rows // 2
     part = half // chips
-    piece = part // n_dp
     halves = flat.reshape(2, half, width)
     mine = jnp.where(core == 0, halves[0], halves[1])
     other = jnp.where(core == 0, halves[1], halves[0])
     s1 = mine + lax.ppermute(other, "ctx", pairs)
     a = a2a(s1.reshape(chips, part, width), "ctx", groups).sum(0)
-    b = a2a(a.reshape(n_dp, piece, width), "dp").sum(0)
-    c = a2a(jnp.broadcast_to(b[None], (n_dp, piece, width)), "dp").reshape(part, width)
+    c = a
+    step = 1
+    while step < n_dp:
+        c = c + lax.ppermute(c, "dp", [(i, i ^ step) for i in range(n_dp)])
+        step *= 2
     d = a2a(jnp.broadcast_to(c[None], (chips, part, width)), "ctx", groups).reshape(half, width)
     e = lax.ppermute(d, "ctx", pairs)
     return jnp.where(core == 0, jnp.concatenate([d, e]), jnp.concatenate([e, d]))

time: 418 us -> 415 us (level)
  blocking collectives: 154 us -> 135 us
  waiting for transfers between devices: 93.4 us -> 104 us
  starting transfers between devices: 21 us -> 26.6 us
    all_to_all x5 -> x3, blocking collectives: 154 us -> 135 us  [a2a(): return lax.all_to_all(x, axis, 0, 0, tiled=True, axis_index_groups=groups)]
    ppermute x0 -> x3, waiting for transfers between devices: none -> 10.4 us  [all_reduce_a2a(): c = c + lax.ppermute(c, 'dp', [(i, i ^ step) for i in range(n_dp)])]
    ppermute x0 -> x3, starting transfers between devices: none -> 5.86 us  [all_reduce_a2a(): c = c + lax.ppermute(c, 'dp', [(i, i ^ step) for i in range(n_dp)])]
  transfers between devices with their start and end apart: 5 -> 8, of which waited for: 4 -> 7; matrix products, arithmetic and copies ran while one was open for 9% -> 9% of each run, Pallas kernels for 0% -> 0%
where the time goes in v2:
time: 415 us; the launch traced here: 414 us
  blocking collectives  135 us (33%)
  waiting for transfers between devices  104 us (25%)
  local copies, waits for them, and re-layouts  67.7 us (16%)
  matrix products  49 us (12%)
  starting transfers between devices  26.6 us (6%)
  Pallas kernels  26.5 us (6%)
  other arithmetic  4.17 us (1%)
    all_to_all x3, blocking collectives, a2a(): return lax.all_to_all(x, axis, 0, 0, tiled=True, axis_index_groups=groups)  135 us
    all_to_all x3, waiting for transfers between devices, a2a(): return lax.all_to_all(x, axis, 0, 0, tiled=True, axis_index_groups=groups)  91.1 us
    pallas_call x1, Pallas kernels, mlp(): pl.pallas_call(mlp_kernel, grid=(rows // tile,), in_specs=[row, row, row,...  26.5 us
    all_to_all x3, starting transfers between devices, a2a(): return lax.all_to_all(x, axis, 0, 0, tiled=True, axis_index_groups=groups)  14.9 us
    ppermute x3, waiting for transfers between devices, all_reduce_a2a(): c = c + lax.ppermute(c, 'dp', [(i, i ^ step) for i in range(n_dp)])  10.4 us
    unnamed x29, local copies, waits for them, and re-layouts  8.72 us
  transfers between devices with their start and end apart: 8, of which 7 were waited for; matrix products, arithmetic and copies ran while one was open for 9% of the time, Pallas kernels for 0%

profile of v2, /device:TPU:1, one launch (start us, length us, event | category | flops | bytes accessed | tf_op | source)
XLA Modules:
  0.0 414.0 jit_solution(15771573004207511766)
XLA Ops:
  10.8 58.7 %all_to_all.30 = bf16[16,32,32,128]{3,2,1,0:T(8,128)(2,1)S(1)} all-to-all(bf16[16,32,32,128]{3,2,1,0:T(8,128)(2,1)S(1)} %copy.51), channel_id=1, replica_groups=mesh['dp'=8,'ctx'=16] {'ctx'}, dimensions={0} | all-to-all | bytes 8388608 | tf_op jit(solution)/shard_map/all_to_all | solution.py:62
  71.5 6.1 %convert_bitcast_fusion.2 = bf16[512,32,128]{0,2,1:T(8,128)(2,1)} fusion(bf16[512,32,128]{2,1,0:T(8,128)(2,1)S(1)} %bitcast.85, bf16[512,512]{1,0:T(8,128)(2,1)S(1)} %copy-done), kind=kOutput, calls=%fused_computation.12 | convolution fusion | flops 2149580800 | bytes 8912896 | tf_op jit(solution)/shard_map/ikc,im->mkc/dot_general | solution.py:120
  77.6 8.0 %copy.53 = bf16[512,32,128]{2,1,0:T(8,128)(2,1)} copy(bf16[512,32,128]{0,2,1:T(8,128)(2,1)} %convert_bitcast_fusion.2) | data formatting | bytes 8388608 | tf_op jit(solution)/shard_map/convert_element_type | solution.py:120
  85.6 5.7 %all-to-all-start.1 = ((bf16[16,32,32,128]{3,2,1,0:T(8,128)(2,1)}), bf16[16,32,32,128]{3,2,1,0:T(8,128)(2,1)}, u32[]{:S(2)}, u32[]{:S(2)}) async-start(bf16[16,32,32,128]{3,2,1,0:T(8,128)(2,1)} %bitcast.88), calls=%async_computation.1 | async-start | bytes 8388608 | tf_op jit(solution)/shard_map/all_to_all | solution.py:62
  93.4 5.5 %copy.49 = bf16[32,16,32,128]{3,2,0,1:T(8,128)(2,1)} copy(bf16[32,16,32,128]{3,2,1,0:T(8,128)(2,1)} %bitcast.96) | data formatting | bytes 8388608 | tf_op jit(solution)/shard_map/squeeze;reshape;squeeze | solution.py:124
  102.0 40.3 %all-to-all-done.1 = bf16[16,32,32,128]{3,2,1,0:T(8,128)(2,1)} async-done(((bf16[16,32,32,128]{3,2,1,0:T(8,128)(2,1)}), bf16[16,32,32,128]{3,2,1,0:T(8,128)(2,1)}, u32[]{:S(2)}, u32[]{:S(2)}) %all-to-all-start.1) | async-done | bytes 4194336 | tf_op jit(solution)/shard_map/all_to_all | solution.py:62
  142.3 26.5 %shard_map.126 = (bf16[16384,128]{1,0:T(8,128)(2,1)}, bf16[16384,128]{1,0:T(8,128)(2,1)}, bf16[16384,128]{1,0:T(8,128)(2,1)}, bf16[16384,128]{1,0:T(8,128)(2,1)}...) custom-call(bf16[16384,128]{1,0:T(8,128)(2,1)} %bitcast.84, bf16[16384,128]{1,0:T(8,128)(2,1)} %bitcast.83, ...), custom_call_target="tpu_custom_call" | custom-call | tf_op jit(solution)/shard_map/pallas_call | solution.py:49
  168.8 55.1 %all_to_all.31 = bf16[16,32,32,128]{3,2,1,0:T(8,128)(2,1)S(1)} all-to-all(bf16[16,32,32,128]{3,2,1,0:T(8,128)(2,1)} %bitcast.106), channel_id=1, replica_groups=mesh['dp'=8,'ctx'=16] {'ctx'}, dimensions={0} | all-to-all | bytes 8388608 | tf_op jit(solution)/shard_map/all_to_all | solution.py:62
  225.9 6.4 %convert_bitcast_fusion.1 = bf16[512,32,128]{0,2,1:T(8,128)(2,1)} fusion(bf16[512,32,128]{2,1,0:T(8,128)(2,1)S(1)} %bitcast.104, bf16[512,512]{1,0:T(8,128)(2,1)S(1)} %copy-done), kind=kOutput, calls=%fused_computation.11 | convolution fusion | flops 2149580800 | bytes 8912896 | tf_op jit(solution)/shard_map/mkc,im->ikc/dot_general | solution.py:130
  232.3 7.8 %copy.60 = bf16[512,32,128]{2,1,0:T(8,128)(2,1)} copy(bf16[512,32,128]{0,2,1:T(8,128)(2,1)} %convert_bitcast_fusion.1) | data formatting | bytes 8388608 | tf_op jit(solution)/shard_map/convert_element_type | solution.py:130
  240.1 5.7 %all-to-all-start.3 = ((bf16[16,32,32,128]{3,2,1,0:T(8,128)(2,1)}), bf16[16,32,32,128]{3,2,1,0:T(8,128)(2,1)}, u32[]{:S(2)}, u32[]{:S(2)}) async-start(bf16[16,32,32,128]{3,2,1,0:T(8,128)(2,1)} %bitcast.87), calls=%async_computation.3 | async-start | bytes 8388608 | tf_op jit(solution)/shard_map/all_to_all | solution.py:62
  245.8 5.5 %copy.58 = bf16[16,32,1,32,128]{4,3,0,1,2:T(8,128)(2,1)} copy(bf16[16,32,1,32,128]{4,3,1,0,2:T(8,128)(2,1)} %bitcast.102) | data formatting | bytes 8388608 | tf_op jit(solution)/shard_map/convert_element_type | solution.py:148
  256.1 40.7 %all-to-all-done.3 = bf16[16,32,32,128]{3,2,1,0:T(8,128)(2,1)} async-done(((bf16[16,32,32,128]{3,2,1,0:T(8,128)(2,1)}), bf16[16,32,32,128]{3,2,1,0:T(8,128)(2,1)}, u32[]{:S(2)}, u32[]{:S(2)}) %all-to-all-start.3) | async-done | bytes 4194336 | tf_op jit(solution)/shard_map/all_to_all | solution.py:62
  296.8 6.6 %fusion.3 = bf16[32,512,128]{1,2,0:T(8,128)(2,1)} fusion(bf16[16,32,32,128]{3,2,1,0:T(8,128)(2,1)} %all-to-all-done.3, bf16[512,16,32,1]{0,2,3,1:T(8,128)(2,1)S(1)} %bitcast.108), kind=kOutput, calls=%fused_computation.8 | convolution fusion | flops 2149580800 | bytes 8912896 | tf_op jit(solution)/shard_map/dirc,jdr->ijc/dot_general | solution.py:135
  303.4 6.5 %copy.62 = bf16[32,512,128]{2,1,0:T(8,128)(2,1)} copy(bf16[32,512,128]{1,2,0:T(8,128)(2,1)} %fusion.3) | data formatting | bytes 8388608 | tf_op jit(solution)/shard_map/dirc,jdr->ijc/transpose | solution.py:135
  309.9 5.8 %convolution_bitcast_fusion = f32[512,16,32]{0,2,1:T(8,128)S(1)} fusion(bf16[32,512,128,1]{2,1,0,3:T(8,128)(2,1)} %bitcast.91, bf16[16,32,32,128]{3,2,1,0:T(8,128)(2,1)} %all-to-all-done.3), kind=kOutput, calls=%fused_computation.24 | convolution fusion | flops 2147483648 | bytes 9437184 | tf_op jit(solution)/shard_map/ijc,dirc->jdr/dot_general | solution.py:136
  322.7 7.1 %fusion.23 = f32[128,256]{0,1:T(8,128)S(1)} fusion(bf16[1,16384,128]{2,1,0:T(8,128)(2,1)} %param.7, bf16[16384,128]{1,0:T(8,128)(2,1)} %bitcast.100, bf16[16384,128]{1,0:T(8,128)(2,1)} %bitcast.98), kind=kOutput, calls=%fused_computation.30 | convolution fusion | flops 1090519040 | bytes 12713984 | tf_op jit(solution)/shard_map/dot_general | solution.py:149
  333.9 21.3 %all_to_all.32 = f32[8,304,128]{2,1,0:T(8,128)S(1)} all-to-all(f32[8,304,128]{2,1,0:T(8,128)S(1)} %bitcast.94), channel_id=1, replica_groups={{0,2,4,6,8,10,12,14},{1,3,5,7,9,11,13,15},{16,18,20,22,24,26,28,30},{17..., dimensions={0} | all-to-all | bytes 2490368 | tf_op jit(solution)/shard_map/all_to_all | solution.py:62
  355.6 3.8 collective-permute-done.1
  367.5 4.0 collective-permute-done.3
  376.2 5.5 %copy.56 = bf16[32,16,1,32,128]{4,3,1,0,2:T(8,128)(2,1)} copy(bf16[32,16,1,32,128]{4,3,0,1,2:T(8,128)(2,1)} %bitcast.97) | data formatting | bytes 8388608 | tf_op jit(solution)/shard_map/transpose | solution.py:142
  381.7 10.0 %all-to-all-done.5 = f32[8,304,128]{2,1,0:T(8,128)S(1)} async-done(((f32[8,304,128]{2,1,0:T(8,128)}), f32[8,304,128]{2,1,0:T(8,128)S(1)}, u32[]{:S(2)}, u32[]{:S(2)}) %all-to-all-start.5) | async-done | bytes 1245216 | tf_op jit(solution)/shard_map/all_to_all | solution.py:62
  391.7 4.7 %collective-permute-start.4 = (f32[2432,128]{1,0:T(8,128)S(1)}, f32[2432,128]{1,0:T(8,128)S(1)}, u32[]{:S(2)}, u32[]{:S(2)}) collective-permute-start(f32[2432,128]{1,0:T(8,128)S(1)} %bitcast.92), channel_id=1, source_target_pairs={{0,1},{1,0},{2,3},{3,2},{4,5},{5,4},{6,7},{7,6},{8,9},{9,8},{10,11... | collective-permute-start | bytes 3735560 | tf_op jit(solution)/shard_map/ppermute | solution.py:86
  401.2 7.9 %fusion.1 = bf16[1,16384,128]{2,1,0:T(8,128)(2,1)} fusion(f32[16384,128]{1,0:T(8,128)S(1)} %bitcast.89, bf16[128,256]{1,0:T(8,128)(2,1)S(1)} %copy-done.12, bf16[16384,128]{1,0:T(8,128)(2,1)} %bitcast.101, bf16[16384,128]{1,0:T(8,128)(2,1)} %bitcast.99), kind=kOutput, calls=%fused_computation.3 | convolution fusion | flops 1094713344 | bytes 21037056 | tf_op jit(solution)/shard_map/dot_general | solution.py:151
  (65 shorter events, 58.0 us)
Async XLA Ops:
  0.6 70.9 %copy-start = (bf16[512,512]{1,0:T(8,128)(2,1)S(1)}, bf16[512,512]{1,0:T(8,128)(2,1)}, u32[]{:S(2)}) copy-start(bf16[512,512]{1,0:T(8,128)(2,1)} %param.11) | copy-start | bytes 1572868
  5.4 1.9 copy-start.5
  69.5 2.0 copy-start.3
  85.6 5.7 %copy-start.12 = (bf16[128,256]{1,0:T(8,128)(2,1)S(1)}, bf16[128,256]{1,0:T(8,128)(2,1)}, u32[]{:S(2)}) copy-start(bf16[128,256]{1,0:T(8,128)(2,1)} %param.9) | copy-start | bytes 196612
  85.6 6.3 %copy-start.9 = (bf16[128,256]{1,0:T(8,128)(2,1)S(1)}, bf16[128,256]{1,0:T(8,128)(2,1)}, u32[]{:S(2)}) copy-start(bf16[128,256]{1,0:T(8,128)(2,1)} %wu_ref.1) | copy-start | bytes 196612
  85.6 7.1 %copy-start.10 = (bf16[256,128]{1,0:T(8,128)(2,1)S(1)}, bf16[256,128]{1,0:T(8,128)(2,1)}, u32[]{:S(2)}) copy-start(bf16[256,128]{1,0:T(8,128)(2,1)} %wd_ref.1) | copy-start | bytes 196612
  85.6 56.7 %all-to-all-start.1 = ((bf16[16,32,32,128]{3,2,1,0:T(8,128)(2,1)}), bf16[16,32,32,128]{3,2,1,0:T(8,128)(2,1)}, u32[]{:S(2)}, u32[]{:S(2)}) async-start(bf16[16,32,32,128]{3,2,1,0:T(8,128)(2,1)} %bitcast.88), calls=%async_computation.1 | async-start | bytes 8388608 | tf_op jit(solution)/shard_map/all_to_all | solution.py:62
  93.4 5.5 %copy-start.2 = (bf16[1,16384,128]{2,1,0:T(8,128)(2,1)S(1)}, bf16[1,16384,128]{2,1,0:T(8,128)(2,1)}, u32[]{:S(2)}) copy-start(bf16[1,16384,128]{2,1,0:T(8,128)(2,1)} %param.7) | copy-start | bytes 12582916
  224.0 1.9 copy-start.6
  240.1 5.7 %copy-start.11 = (f32[128,256]{1,0:T(8,128)S(1)}, f32[128,256]{1,0:T(8,128)}, u32[]{:S(2)}) copy-start(f32[128,256]{1,0:T(8,128)} %get-tuple-element.17) | copy-start | bytes 393220
  240.1 56.7 %all-to-all-start.3 = ((bf16[16,32,32,128]{3,2,1,0:T(8,128)(2,1)}), bf16[16,32,32,128]{3,2,1,0:T(8,128)(2,1)}, u32[]{:S(2)}, u32[]{:S(2)}) async-start(bf16[16,32,32,128]{3,2,1,0:T(8,128)(2,1)} %bitcast.87), calls=%async_computation.3 | async-start | bytes 8388608 | tf_op jit(solution)/shard_map/all_to_all | solution.py:62
  245.8 5.6 %copy-start.4 = (bf16[16,32,32,128]{3,2,1,0:T(8,128)(2,1)S(1)}, bf16[16,32,32,128]{3,2,1,0:T(8,128)(2,1)}, u32[]{:S(2)}) copy-start(bf16[16,32,32,128]{3,2,1,0:T(8,128)(2,1)} %copy-done.3) | copy-start | bytes 12582916
  245.8 5.6 %copy-start.7 = (bf16[16,32,32,128]{3,2,1,0:T(8,128)(2,1)S(1)}, bf16[16,32,32,128]{3,2,1,0:T(8,128)(2,1)}, u32[]{:S(2)}) copy-start(bf16[16,32,32,128]{3,2,1,0:T(8,128)(2,1)} %copy-done.6) | copy-start | bytes 12582916
  322.7 7.2 %copy-start.8 = (f32[256,128]{1,0:T(8,128)S(1)}, f32[256,128]{1,0:T(8,128)}, u32[]{:S(2)}) copy-start(f32[256,128]{1,0:T(8,128)} %get-tuple-element.18) | copy-start | bytes 393220
  330.0 3.7 collective-permute-start
  355.2 4.2 %collective-permute-start.1 = (f32[304,128]{1,0:T(8,128)S(1)}, f32[304,128]{1,0:T(8,128)S(1)}, u32[]{:S(2)}, u32[]{:S(2)}) collective-permute-start(f32[304,128]{1,0:T(8,128)S(1)} %reduce_sum.9), channel_id=1, source_target_pairs={{0,16},{16,0},{32,48},{48,32},{64,80},{80,64},{96,112},{112,96},{1... | collective-permute-start | bytes 466952 | tf_op jit(solution)/shard_map/ppermute | solution.py:83
  359.4 4.6 %collective-permute-start.2 = (f32[304,128]{1,0:T(8,128)S(1)}, f32[304,128]{1,0:T(8,128)S(1)}, u32[]{:S(2)}, u32[]{:S(2)}) collective-permute-start(f32[304,128]{1,0:T(8,128)S(1)} %add.22), channel_id=1, source_target_pairs={{0,32},{16,48},{32,0},{48,16},{64,96},{80,112},{96,64},{112,80},{1... | collective-permute-start | bytes 466952 | tf_op jit(solution)/shard_map/ppermute | solution.py:83
  364.0 7.5 %collective-permute-start.3 = (f32[304,128]{1,0:T(8,128)S(1)}, f32[304,128]{1,0:T(8,128)S(1)}, u32[]{:S(2)}, u32[]{:S(2)}) collective-permute-start(f32[304,128]{1,0:T(8,128)S(1)} %add.23), channel_id=1, source_target_pairs={{0,64},{16,80},{32,96},{48,112},{64,0},{80,16},{96,32},{112,48},{1... | collective-permute-start | bytes 466952 | tf_op jit(solution)/shard_map/ppermute | solution.py:83
  372.6 19.1 %all-to-all-start.5 = ((f32[8,304,128]{2,1,0:T(8,128)}), f32[8,304,128]{2,1,0:T(8,128)S(1)}, u32[]{:S(2)}, u32[]{:S(2)}) async-start(f32[8,304,128]{2,1,0:T(8,128)} %broadcast_in_dim.10), calls=%async_computation.5 | async-start | bytes 2490368 | tf_op jit(solution)/shard_map/all_to_all | solution.py:62
  391.7 17.5 %collective-permute-start.4 = (f32[2432,128]{1,0:T(8,128)S(1)}, f32[2432,128]{1,0:T(8,128)S(1)}, u32[]{:S(2)}, u32[]{:S(2)}) collective-permute-start(f32[2432,128]{1,0:T(8,128)S(1)} %bitcast.92), channel_id=1, source_target_pairs={{0,1},{1,0},{2,3},{3,2},{4,5},{5,4},{6,7},{7,6},{8,9},{9,8},{10,11... | collective-permute-start | bytes 3735560 | tf_op jit(solution)/shard_map/ppermute | solution.py:86
  409.5 4.5 %copy-start.1 = (bf16[512,512]{1,0:T(8,128)(2,1)S(1)}, bf16[512,512]{1,0:T(8,128)(2,1)}, u32[]{:S(2)}) copy-start(bf16[512,512]{1,0:T(8,128)(2,1)} %param.11) | copy-start | bytes 1572868

commit v3 on v2

--- a/solution.py
+++ b/solution.py
@@ -76,7 +76,15 @@
     mine = jnp.where(core == 0, halves[0], halves[1])
     other = jnp.where(core == 0, halves[1], halves[0])
     s1 = mine + lax.ppermute(other, "ctx", pairs)
-    a = a2a(s1.reshape(chips, part, width), "ctx", groups).sum(0)
+    chip = lax.axis_index("ctx") // 2
+    a = s1
+    bit_n = chips.bit_length() - 1
+    for b in reversed(range(bit_n)):
+        n = a.shape[0] // 2
+        upper = (chip >> b) & 1
+        keep = jnp.where(upper == 0, a[:n], a[n:])
+        send = jnp.where(upper == 0, a[n:], a[:n])
+        a = keep + lax.ppermute(send, "ctx", [(i, i ^ (2 << b)) for i in range(n_ctx)])
     c = a
     step = 1
     while step < n_dp:

time: 415 us -> 434 us (1.046); the launches traced: 414 us -> 427 us
  waiting for transfers between devices: 104 us -> 131 us
  blocking collectives: 135 us -> 114 us
  starting transfers between devices: 26.6 us -> 32.3 us
    ppermute x0 -> x3, waiting for transfers between devices: none -> 29 us  [all_reduce_a2a(): lax.ppermute(send, 'ctx', [(i, i ^ 2 << b) for i in range(n_ctx)])]
    all_to_all x3 -> x2, blocking collectives: 135 us -> 114 us  [a2a(): return lax.all_to_all(x, axis, 0, 0, tiled=True, axis_index_groups=groups)]
    unnamed x29 -> x31, local copies, waits for them, and re-layouts: 8.72 us -> 8.71 us
  transfers between devices with their start and end apart: 8 -> 11, of which waited for: 7 -> 10; matrix products, arithmetic and copies ran while one was open for 9% -> 9% of each run, Pallas kernels for 0% -> 0%
where the time goes in v3:
time: 434 us; the launch traced here: 427 us
  waiting for transfers between devices  131 us (30%)
  blocking collectives  114 us (26%)
  local copies, waits for them, and re-layouts  66.4 us (15%)
  matrix products  48.1 us (11%)
  starting transfers between devices  32.3 us (7%)
  Pallas kernels  26.5 us (6%)
  other arithmetic  7.01 us (2%)
    all_to_all x2, blocking collectives, a2a(): return lax.all_to_all(x, axis, 0, 0, tiled=True, axis_index_groups=groups)  114 us
    all_to_all x3, waiting for transfers between devices, a2a(): return lax.all_to_all(x, axis, 0, 0, tiled=True, axis_index_groups=groups)  90.4 us
    ppermute x3, waiting for transfers between devices, all_reduce_a2a(): lax.ppermute(send, 'ctx', [(i, i ^ 2 << b) for i in range(n_ctx)])  29 us
    pallas_call x1, Pallas kernels, mlp(): pl.pallas_call(mlp_kernel, grid=(rows // tile,), in_specs=[row, row, row,...  26.5 us
    all_to_all x3, starting transfers between devices, a2a(): return lax.all_to_all(x, axis, 0, 0, tiled=True, axis_index_groups=groups)  16 us
    ppermute x3, waiting for transfers between devices, all_reduce_a2a(): c = c + lax.ppermute(c, 'dp', [(i, i ^ step) for i in range(n_dp)])  9.03 us
    unnamed x31, local copies, waits for them, and re-layouts  8.71 us
  transfers between devices with their start and end apart: 11, of which 10 were waited for; matrix products, arithmetic and copies ran while one was open for 9% of the time, Pallas kernels for 0%

profile of v3, /device:TPU:1, one launch (start us, length us, event | category | flops | bytes accessed | tf_op | source)
XLA Modules:
  0.0 426.8 jit_solution(14726662439172459588)
XLA Ops:
  10.8 58.7 %all_to_all.25 = bf16[16,32,32,128]{3,2,1,0:T(8,128)(2,1)S(1)} all-to-all(bf16[16,32,32,128]{3,2,1,0:T(8,128)(2,1)S(1)} %copy.51), channel_id=1, replica_groups=mesh['dp'=8,'ctx'=16] {'ctx'}, dimensions={0} | all-to-all | bytes 8388608 | tf_op jit(solution)/shard_map/all_to_all | solution.py:62
  71.5 6.1 %convert_bitcast_fusion.2 = bf16[512,32,128]{0,2,1:T(8,128)(2,1)} fusion(bf16[512,32,128]{2,1,0:T(8,128)(2,1)S(1)} %bitcast.84, bf16[512,512]{1,0:T(8,128)(2,1)S(1)} %copy-done), kind=kOutput, calls=%fused_computation.12 | convolution fusion | flops 2149580800 | bytes 8912896 | tf_op jit(solution)/shard_map/ikc,im->mkc/dot_general | solution.py:128
  77.6 7.9 %copy.53 = bf16[512,32,128]{2,1,0:T(8,128)(2,1)} copy(bf16[512,32,128]{0,2,1:T(8,128)(2,1)} %convert_bitcast_fusion.2) | data formatting | bytes 8388608 | tf_op jit(solution)/shard_map/convert_element_type | solution.py:128
  85.5 6.0 %all-to-all-start.1 = ((bf16[16,32,32,128]{3,2,1,0:T(8,128)(2,1)}), bf16[16,32,32,128]{3,2,1,0:T(8,128)(2,1)}, u32[]{:S(2)}, u32[]{:S(2)}) async-start(bf16[16,32,32,128]{3,2,1,0:T(8,128)(2,1)} %bitcast.87), calls=%async_computation.1 | async-start | bytes 8388608 | tf_op jit(solution)/shard_map/all_to_all | solution.py:62
  93.6 5.5 %copy.49 = bf16[32,16,32,128]{3,2,0,1:T(8,128)(2,1)} copy(bf16[32,16,32,128]{3,2,1,0:T(8,128)(2,1)} %bitcast.94) | data formatting | bytes 8388608 | tf_op jit(solution)/shard_map/squeeze;reshape;squeeze | solution.py:132
  102.2 40.2 %all-to-all-done.1 = bf16[16,32,32,128]{3,2,1,0:T(8,128)(2,1)} async-done(((bf16[16,32,32,128]{3,2,1,0:T(8,128)(2,1)}), bf16[16,32,32,128]{3,2,1,0:T(8,128)(2,1)}, u32[]{:S(2)}, u32[]{:S(2)}) %all-to-all-start.1) | async-done | bytes 4194336 | tf_op jit(solution)/shard_map/all_to_all | solution.py:62
  142.3 26.5 %shard_map.126 = (bf16[16384,128]{1,0:T(8,128)(2,1)}, bf16[16384,128]{1,0:T(8,128)(2,1)}, bf16[16384,128]{1,0:T(8,128)(2,1)}, bf16[16384,128]{1,0:T(8,128)(2,1)}...) custom-call(bf16[16384,128]{1,0:T(8,128)(2,1)} %bitcast.83, bf16[16384,128]{1,0:T(8,128)(2,1)} %bitcast.82, ...), custom_call_target="tpu_custom_call" | custom-call | tf_op jit(solution)/shard_map/pallas_call | solution.py:49
  168.8 55.1 %all_to_all.26 = bf16[16,32,32,128]{3,2,1,0:T(8,128)(2,1)S(1)} all-to-all(bf16[16,32,32,128]{3,2,1,0:T(8,128)(2,1)} %bitcast.104), channel_id=1, replica_groups=mesh['dp'=8,'ctx'=16] {'ctx'}, dimensions={0} | all-to-all | bytes 8388608 | tf_op jit(solution)/shard_map/all_to_all | solution.py:62
  225.9 6.4 %convert_bitcast_fusion.1 = bf16[512,32,128]{0,2,1:T(8,128)(2,1)} fusion(bf16[512,32,128]{2,1,0:T(8,128)(2,1)S(1)} %bitcast.102, bf16[512,512]{1,0:T(8,128)(2,1)S(1)} %copy-done), kind=kOutput, calls=%fused_computation.11 | convolution fusion | flops 2149580800 | bytes 8912896 | tf_op jit(solution)/shard_map/mkc,im->ikc/dot_general | solution.py:138
  232.3 7.8 %copy.60 = bf16[512,32,128]{2,1,0:T(8,128)(2,1)} copy(bf16[512,32,128]{0,2,1:T(8,128)(2,1)} %convert_bitcast_fusion.1) | data formatting | bytes 8388608 | tf_op jit(solution)/shard_map/convert_element_type | solution.py:138
  240.1 6.0 %all-to-all-start.3 = ((bf16[16,32,32,128]{3,2,1,0:T(8,128)(2,1)}), bf16[16,32,32,128]{3,2,1,0:T(8,128)(2,1)}, u32[]{:S(2)}, u32[]{:S(2)}) async-start(bf16[16,32,32,128]{3,2,1,0:T(8,128)(2,1)} %bitcast.86), calls=%async_computation.3 | async-start | bytes 8388608 | tf_op jit(solution)/shard_map/all_to_all | solution.py:62
  246.2 5.6 %copy.58 = bf16[16,32,1,32,128]{4,3,0,1,2:T(8,128)(2,1)} copy(bf16[16,32,1,32,128]{4,3,1,0,2:T(8,128)(2,1)} %bitcast.101) | data formatting | bytes 8388608 | tf_op jit(solution)/shard_map/convert_element_type | solution.py:156
  254.3 42.7 %all-to-all-done.3 = bf16[16,32,32,128]{3,2,1,0:T(8,128)(2,1)} async-done(((bf16[16,32,32,128]{3,2,1,0:T(8,128)(2,1)}), bf16[16,32,32,128]{3,2,1,0:T(8,128)(2,1)}, u32[]{:S(2)}, u32[]{:S(2)}) %all-to-all-start.3) | async-done | bytes 4194336 | tf_op jit(solution)/shard_map/all_to_all | solution.py:62
  297.0 6.6 %fusion.3 = bf16[32,512,128]{1,2,0:T(8,128)(2,1)} fusion(bf16[16,32,32,128]{3,2,1,0:T(8,128)(2,1)} %all-to-all-done.3, bf16[512,16,32,1]{0,2,3,1:T(8,128)(2,1)S(1)} %bitcast.106), kind=kOutput, calls=%fused_computation.8 | convolution fusion | flops 2149580800 | bytes 8912896 | tf_op jit(solution)/shard_map/dirc,jdr->ijc/dot_general | solution.py:143
  303.6 6.5 %copy.62 = bf16[32,512,128]{2,1,0:T(8,128)(2,1)} copy(bf16[32,512,128]{1,2,0:T(8,128)(2,1)} %fusion.3) | data formatting | bytes 8388608 | tf_op jit(solution)/shard_map/dirc,jdr->ijc/transpose | solution.py:143
  310.1 5.8 %convolution_bitcast_fusion = f32[512,16,32]{0,2,1:T(8,128)S(1)} fusion(bf16[32,512,128,1]{2,1,0,3:T(8,128)(2,1)} %bitcast.90, bf16[16,32,32,128]{3,2,1,0:T(8,128)(2,1)} %all-to-all-done.3), kind=kOutput, calls=%fused_computation.24 | convolution fusion | flops 2147483648 | bytes 9437184 | tf_op jit(solution)/shard_map/ijc,dirc->jdr/dot_general | solution.py:144
  322.9 7.1 %fusion.23 = f32[128,256]{0,1:T(8,128)S(1)} fusion(bf16[1,16384,128]{2,1,0:T(8,128)(2,1)} %param.7, bf16[16384,128]{1,0:T(8,128)(2,1)} %bitcast.98, bf16[16384,128]{1,0:T(8,128)(2,1)} %bitcast.96), kind=kOutput, calls=%fused_computation.30 | convolution fusion | flops 1090519040 | bytes 12713984 | tf_op jit(solution)/shard_map/dot_general | solution.py:157
  337.7 16.2 %collective-permute-done.1 = f32[1216,128]{1,0:T(8,128)S(1)} collective-permute-done((f32[1216,128]{1,0:T(8,128)S(1)}, f32[1216,128]{1,0:T(8,128)S(1)}, u32[]{:S(2)}, u32[]{:S(2)}) %collective-permute-start.1) | collective-permute-done | bytes 622624 | tf_op jit(solution)/shard_map/ppermute | solution.py:87
  354.4 7.7 %collective-permute-done.2 = f32[608,128]{1,0:T(8,128)S(1)} collective-permute-done((f32[608,128]{1,0:T(8,128)S(1)}, f32[608,128]{1,0:T(8,128)S(1)}, u32[]{:S(2)}, u32[]{:S(2)}) %collective-permute-start.2) | collective-permute-done | bytes 311328 | tf_op jit(solution)/shard_map/ppermute | solution.py:87
  362.6 5.1 %collective-permute-done.3 = f32[304,128]{1,0:T(8,128)S(1)} collective-permute-done((f32[304,128]{1,0:T(8,128)S(1)}, f32[304,128]{1,0:T(8,128)S(1)}, u32[]{:S(2)}, u32[]{:S(2)}) %collective-permute-start.3) | collective-permute-done | bytes 155680 | tf_op jit(solution)/shard_map/ppermute | solution.py:87
  387.6 5.5 %copy.56 = bf16[32,16,1,32,128]{4,3,1,0,2:T(8,128)(2,1)} copy(bf16[32,16,1,32,128]{4,3,0,1,2:T(8,128)(2,1)} %bitcast.95) | data formatting | bytes 8388608 | tf_op jit(solution)/shard_map/transpose | solution.py:150
  393.1 7.5 %all-to-all-done.4 = f32[8,304,128]{2,1,0:T(8,128)S(1)} async-done(((f32[8,304,128]{2,1,0:T(8,128)}), f32[8,304,128]{2,1,0:T(8,128)S(1)}, u32[]{:S(2)}, u32[]{:S(2)}) %all-to-all-start.4) | async-done | bytes 1245216 | tf_op jit(solution)/shard_map/all_to_all | solution.py:62
  400.6 8.1 %collective-permute-start.7 = (f32[2432,128]{1,0:T(8,128)S(1)}, f32[2432,128]{1,0:T(8,128)S(1)}, u32[]{:S(2)}, u32[]{:S(2)}) collective-permute-start(f32[2432,128]{1,0:T(8,128)S(1)} %bitcast.91), channel_id=1, source_target_pairs={{0,1},{1,0},{2,3},{3,2},{4,5},{5,4},{6,7},{7,6},{8,9},{9,8},{10,11... | collective-permute-start | bytes 3735560 | tf_op jit(solution)/shard_map/ppermute | solution.py:94
  413.5 7.9 %fusion.1 = bf16[1,16384,128]{2,1,0:T(8,128)(2,1)} fusion(f32[16384,128]{1,0:T(8,128)S(1)} %bitcast.88, bf16[128,256]{1,0:T(8,128)(2,1)S(1)} %copy-done.13, bf16[16384,128]{1,0:T(8,128)(2,1)} %bitcast.99, bf16[16384,128]{1,0:T(8,128)(2,1)} %bitcast.97), kind=kOutput, calls=%fused_computation.3 | convolution fusion | flops 1094713344 | bytes 21037056 | tf_op jit(solution)/shard_map/dot_general | solution.py:159
  (77 shorter events, 67.0 us)
Async XLA Ops:
  0.6 70.9 %copy-start = (bf16[512,512]{1,0:T(8,128)(2,1)S(1)}, bf16[512,512]{1,0:T(8,128)(2,1)}, u32[]{:S(2)}) copy-start(bf16[512,512]{1,0:T(8,128)(2,1)} %param.11) | copy-start | bytes 1572868
  5.4 2.0 copy-start.6
  85.5 6.0 %copy-start.13 = (bf16[128,256]{1,0:T(8,128)(2,1)S(1)}, bf16[128,256]{1,0:T(8,128)(2,1)}, u32[]{:S(2)}) copy-start(bf16[128,256]{1,0:T(8,128)(2,1)} %param.9) | copy-start | bytes 196612
  85.5 6.6 %copy-start.10 = (bf16[128,256]{1,0:T(8,128)(2,1)S(1)}, bf16[128,256]{1,0:T(8,128)(2,1)}, u32[]{:S(2)}) copy-start(bf16[128,256]{1,0:T(8,128)(2,1)} %wu_ref.1) | copy-start | bytes 196612
  85.5 7.4 %copy-start.11 = (bf16[256,128]{1,0:T(8,128)(2,1)S(1)}, bf16[256,128]{1,0:T(8,128)(2,1)}, u32[]{:S(2)}) copy-start(bf16[256,128]{1,0:T(8,128)(2,1)} %wd_ref.1) | copy-start | bytes 196612
  85.5 56.9 %all-to-all-start.1 = ((bf16[16,32,32,128]{3,2,1,0:T(8,128)(2,1)}), bf16[16,32,32,128]{3,2,1,0:T(8,128)(2,1)}, u32[]{:S(2)}, u32[]{:S(2)}) async-start(bf16[16,32,32,128]{3,2,1,0:T(8,128)(2,1)} %bitcast.87), calls=%async_computation.1 | async-start | bytes 8388608 | tf_op jit(solution)/shard_map/all_to_all | solution.py:62
  93.6 5.5 %copy-start.2 = (bf16[1,16384,128]{2,1,0:T(8,128)(2,1)S(1)}, bf16[1,16384,128]{2,1,0:T(8,128)(2,1)}, u32[]{:S(2)}) copy-start(bf16[1,16384,128]{2,1,0:T(8,128)(2,1)} %param.7) | copy-start | bytes 12582916
  224.0 2.0 copy-start.7
  240.1 6.1 %copy-start.12 = (f32[128,256]{1,0:T(8,128)S(1)}, f32[128,256]{1,0:T(8,128)}, u32[]{:S(2)}) copy-start(f32[128,256]{1,0:T(8,128)} %get-tuple-element.17) | copy-start | bytes 393220
  240.1 56.9 %all-to-all-start.3 = ((bf16[16,32,32,128]{3,2,1,0:T(8,128)(2,1)}), bf16[16,32,32,128]{3,2,1,0:T(8,128)(2,1)}, u32[]{:S(2)}, u32[]{:S(2)}) async-start(bf16[16,32,32,128]{3,2,1,0:T(8,128)(2,1)} %bitcast.86), calls=%async_computation.3 | async-start | bytes 8388608 | tf_op jit(solution)/shard_map/all_to_all | solution.py:62
  246.2 5.6 %copy-start.4 = (bf16[16,32,32,128]{3,2,1,0:T(8,128)(2,1)S(1)}, bf16[16,32,32,128]{3,2,1,0:T(8,128)(2,1)}, u32[]{:S(2)}) copy-start(bf16[16,32,32,128]{3,2,1,0:T(8,128)(2,1)} %copy-done.3) | copy-start | bytes 12582916
  246.2 5.6 %copy-start.8 = (bf16[16,32,32,128]{3,2,1,0:T(8,128)(2,1)S(1)}, bf16[16,32,32,128]{3,2,1,0:T(8,128)(2,1)}, u32[]{:S(2)}) copy-start(bf16[16,32,32,128]{3,2,1,0:T(8,128)(2,1)} %copy-done.7) | copy-start | bytes 12582916
  254.3 75.8 %copy-start.5 = (f32[2048,128]{1,0:T(8,128)}, f32[2048,128]{1,0:T(8,128)S(1)}, u32[]{:S(2)}) copy-start(f32[2048,128]{1,0:T(8,128)S(1)} %reshape.96) | copy-start | bytes 3145732
  322.9 7.2 %copy-start.9 = (f32[256,128]{1,0:T(8,128)S(1)}, f32[256,128]{1,0:T(8,128)}, u32[]{:S(2)}) copy-start(f32[256,128]{1,0:T(8,128)} %get-tuple-element.18) | copy-start | bytes 393220
  331.3 3.9 collective-permute-start
  337.1 16.8 %collective-permute-start.1 = (f32[1216,128]{1,0:T(8,128)S(1)}, f32[1216,128]{1,0:T(8,128)S(1)}, u32[]{:S(2)}, u32[]{:S(2)}) collective-permute-start(f32[1216,128]{1,0:T(8,128)S(1)} %slice_select_fusion), channel_id=1, source_target_pairs={{0,8},{1,9},{2,10},{3,11},{4,12},{5,13},{6,14},{7,15},{8,0},{9,1},... | collective-permute-start | bytes 1867784 | tf_op jit(solution)/shard_map/ppermute | solution.py:87
  354.0 8.0 %collective-permute-start.2 = (f32[608,128]{1,0:T(8,128)S(1)}, f32[608,128]{1,0:T(8,128)S(1)}, u32[]{:S(2)}, u32[]{:S(2)}) collective-permute-start(f32[608,128]{1,0:T(8,128)S(1)} %slice_select_fusion.1), channel_id=1, source_target_pairs={{0,4},{1,5},{2,6},{3,7},{4,0},{5,1},{6,2},{7,3},{8,12},{9,13},{10,... | collective-permute-start | bytes 933896 | tf_op jit(solution)/shard_map/ppermute | solution.py:87
  362.1 5.7 %collective-permute-start.3 = (f32[304,128]{1,0:T(8,128)S(1)}, f32[304,128]{1,0:T(8,128)S(1)}, u32[]{:S(2)}, u32[]{:S(2)}) collective-permute-start(f32[304,128]{1,0:T(8,128)S(1)} %slice_select_fusion.2), channel_id=1, source_target_pairs={{0,2},{1,3},{2,0},{3,1},{4,6},{5,7},{6,4},{7,5},{8,10},{9,11},{10,... | collective-permute-start | bytes 466952 | tf_op jit(solution)/shard_map/ppermute | solution.py:87
  367.8 4.2 collective-permute-start.4
  372.0 4.3 %collective-permute-start.5 = (f32[304,128]{1,0:T(8,128)S(1)}, f32[304,128]{1,0:T(8,128)S(1)}, u32[]{:S(2)}, u32[]{:S(2)}) collective-permute-start(f32[304,128]{1,0:T(8,128)S(1)} %add.35), channel_id=1, source_target_pairs={{0,32},{16,48},{32,0},{48,16},{64,96},{80,112},{96,64},{112,80},{1... | collective-permute-start | bytes 466952 | tf_op jit(solution)/shard_map/ppermute | solution.py:91
  376.3 6.2 %collective-permute-start.6 = (f32[304,128]{1,0:T(8,128)S(1)}, f32[304,128]{1,0:T(8,128)S(1)}, u32[]{:S(2)}, u32[]{:S(2)}) collective-permute-start(f32[304,128]{1,0:T(8,128)S(1)} %add.36), channel_id=1, source_target_pairs={{0,64},{16,80},{32,96},{48,112},{64,0},{80,16},{96,32},{112,48},{1... | collective-permute-start | bytes 466952 | tf_op jit(solution)/shard_map/ppermute | solution.py:91
  383.6 17.0 %all-to-all-start.4 = ((f32[8,304,128]{2,1,0:T(8,128)}), f32[8,304,128]{2,1,0:T(8,128)S(1)}, u32[]{:S(2)}, u32[]{:S(2)}) async-start(f32[8,304,128]{2,1,0:T(8,128)} %broadcast_in_dim.10), calls=%async_computation.4 | async-start | bytes 2490368 | tf_op jit(solution)/shard_map/all_to_all | solution.py:62
  400.6 20.9 %collective-permute-start.7 = (f32[2432,128]{1,0:T(8,128)S(1)}, f32[2432,128]{1,0:T(8,128)S(1)}, u32[]{:S(2)}, u32[]{:S(2)}) collective-permute-start(f32[2432,128]{1,0:T(8,128)S(1)} %bitcast.91), channel_id=1, source_target_pairs={{0,1},{1,0},{2,3},{3,2},{4,5},{5,4},{6,7},{7,6},{8,9},{9,8},{10,11... | collective-permute-start | bytes 3735560 | tf_op jit(solution)/shard_map/ppermute | solution.py:94
  421.8 4.5 %copy-start.1 = (bf16[512,512]{1,0:T(8,128)(2,1)S(1)}, bf16[512,512]{1,0:T(8,128)(2,1)}, u32[]{:S(2)}) copy-start(bf16[512,512]{1,0:T(8,128)(2,1)} %param.11) | copy-start | bytes 1572868
  (1 other events, 2.0 us)

commit v4 on v2

--- a/solution.py
+++ b/solution.py
@@ -39,7 +39,7 @@
     dm_ref[...] = (dh32 * gate).astype(bf16)
     dg_ref[...] = (dh32 * mixed32 * gate * (1.0 - gate)).astype(bf16)
 
-def mlp(x, cot, mixed, w_gate, w_up, w_down, tile=1024):
+def mlp(x, cot, mixed, w_gate, w_up, w_down, tile=2048):
     rows, width = x.shape
     ff = w_up.shape[1]
     f32 = jnp.float32

time: 415 us -> 420 us (1.012); the launches traced: 414 us -> 412 us
  no operation moved by 1% of the time
where the time goes in v4:
time: 420 us; the launch traced here: 412 us
  blocking collectives  135 us (32%)
  waiting for transfers between devices  104 us (25%)
  local copies, waits for them, and re-layouts  67.7 us (16%)
  matrix products  49 us (12%)
  starting transfers between devices  27.3 us (6%)
  Pallas kernels  24 us (6%)
    all_to_all x3, blocking collectives, a2a(): return lax.all_to_all(x, axis, 0, 0, tiled=True, axis_index_groups=groups)  135 us
    all_to_all x3, waiting for transfers between devices, a2a(): return lax.all_to_all(x, axis, 0, 0, tiled=True, axis_index_groups=groups)  90.7 us
    pallas_call x1, Pallas kernels, mlp(): pl.pallas_call(mlp_kernel, grid=(rows // tile,), in_specs=[row, row, row,...  24 us
    all_to_all x3, starting transfers between devices, a2a(): return lax.all_to_all(x, axis, 0, 0, tiled=True, axis_index_groups=groups)  15.6 us
    ppermute x3, waiting for transfers between devices, all_reduce_a2a(): c = c + lax.ppermute(c, 'dp', [(i, i ^ step) for i in range(n_dp)])  10.4 us
    unnamed x29, local copies, waits for them, and re-layouts  8.72 us
  transfers between devices with their start and end apart: 8, of which 7 were waited for; matrix products, arithmetic and copies ran while one was open for 9% of the time, Pallas kernels for 0%

profile of v4, /device:TPU:1, one launch (start us, length us, event | category | flops | bytes accessed | tf_op | source)
XLA Modules:
  0.0 412.3 jit_solution(9406780291905793985)
XLA Ops:
  10.8 58.7 %all_to_all.30 = bf16[16,32,32,128]{3,2,1,0:T(8,128)(2,1)S(1)} all-to-all(bf16[16,32,32,128]{3,2,1,0:T(8,128)(2,1)S(1)} %copy.51), channel_id=1, replica_groups=mesh['dp'=8,'ctx'=16] {'ctx'}, dimensions={0} | all-to-all | bytes 8388608 | tf_op jit(solution)/shard_map/all_to_all | solution.py:62
  71.5 6.1 %convert_bitcast_fusion.2 = bf16[512,32,128]{0,2,1:T(8,128)(2,1)} fusion(bf16[512,32,128]{2,1,0:T(8,128)(2,1)S(1)} %bitcast.85, bf16[512,512]{1,0:T(8,128)(2,1)S(1)} %copy-done), kind=kOutput, calls=%fused_computation.12 | convolution fusion | flops 2149580800 | bytes 8912896 | tf_op jit(solution)/shard_map/ikc,im->mkc/dot_general | solution.py:120
  77.6 8.0 %copy.53 = bf16[512,32,128]{2,1,0:T(8,128)(2,1)} copy(bf16[512,32,128]{0,2,1:T(8,128)(2,1)} %convert_bitcast_fusion.2) | data formatting | bytes 8388608 | tf_op jit(solution)/shard_map/convert_element_type | solution.py:120
  85.6 6.0 %all-to-all-start.1 = ((bf16[16,32,32,128]{3,2,1,0:T(8,128)(2,1)}), bf16[16,32,32,128]{3,2,1,0:T(8,128)(2,1)}, u32[]{:S(2)}, u32[]{:S(2)}) async-start(bf16[16,32,32,128]{3,2,1,0:T(8,128)(2,1)} %bitcast.88), calls=%async_computation.1 | async-start | bytes 8388608 | tf_op jit(solution)/shard_map/all_to_all | solution.py:62
  93.7 5.5 %copy.49 = bf16[32,16,32,128]{3,2,0,1:T(8,128)(2,1)} copy(bf16[32,16,32,128]{3,2,1,0:T(8,128)(2,1)} %bitcast.96) | data formatting | bytes 8388608 | tf_op jit(solution)/shard_map/squeeze;reshape;squeeze | solution.py:124
  102.3 40.2 %all-to-all-done.1 = bf16[16,32,32,128]{3,2,1,0:T(8,128)(2,1)} async-done(((bf16[16,32,32,128]{3,2,1,0:T(8,128)(2,1)}), bf16[16,32,32,128]{3,2,1,0:T(8,128)(2,1)}, u32[]{:S(2)}, u32[]{:S(2)}) %all-to-all-start.1) | async-done | bytes 4194336 | tf_op jit(solution)/shard_map/all_to_all | solution.py:62
  142.5 24.0 %shard_map.126 = (bf16[16384,128]{1,0:T(8,128)(2,1)}, bf16[16384,128]{1,0:T(8,128)(2,1)}, bf16[16384,128]{1,0:T(8,128)(2,1)}, bf16[16384,128]{1,0:T(8,128)(2,1)}...) custom-call(bf16[16384,128]{1,0:T(8,128)(2,1)} %bitcast.84, bf16[16384,128]{1,0:T(8,128)(2,1)} %bitcast.83, ...), custom_call_target="tpu_custom_call" | custom-call | tf_op jit(solution)/shard_map/pallas_call | solution.py:49
  166.4 55.1 %all_to_all.31 = bf16[16,32,32,128]{3,2,1,0:T(8,128)(2,1)S(1)} all-to-all(bf16[16,32,32,128]{3,2,1,0:T(8,128)(2,1)} %bitcast.106), channel_id=1, replica_groups=mesh['dp'=8,'ctx'=16] {'ctx'}, dimensions={0} | all-to-all | bytes 8388608 | tf_op jit(solution)/shard_map/all_to_all | solution.py:62
  223.5 6.4 %convert_bitcast_fusion.1 = bf16[512,32,128]{0,2,1:T(8,128)(2,1)} fusion(bf16[512,32,128]{2,1,0:T(8,128)(2,1)S(1)} %bitcast.104, bf16[512,512]{1,0:T(8,128)(2,1)S(1)} %copy-done), kind=kOutput, calls=%fused_computation.11 | convolution fusion | flops 2149580800 | bytes 8912896 | tf_op jit(solution)/shard_map/mkc,im->ikc/dot_general | solution.py:130
  229.9 7.8 %copy.60 = bf16[512,32,128]{2,1,0:T(8,128)(2,1)} copy(bf16[512,32,128]{0,2,1:T(8,128)(2,1)} %convert_bitcast_fusion.1) | data formatting | bytes 8388608 | tf_op jit(solution)/shard_map/convert_element_type | solution.py:130
  237.7 6.0 %all-to-all-start.3 = ((bf16[16,32,32,128]{3,2,1,0:T(8,128)(2,1)}), bf16[16,32,32,128]{3,2,1,0:T(8,128)(2,1)}, u32[]{:S(2)}, u32[]{:S(2)}) async-start(bf16[16,32,32,128]{3,2,1,0:T(8,128)(2,1)} %bitcast.87), calls=%async_computation.3 | async-start | bytes 8388608 | tf_op jit(solution)/shard_map/all_to_all | solution.py:62
  243.8 5.5 %copy.58 = bf16[16,32,1,32,128]{4,3,0,1,2:T(8,128)(2,1)} copy(bf16[16,32,1,32,128]{4,3,1,0,2:T(8,128)(2,1)} %bitcast.102) | data formatting | bytes 8388608 | tf_op jit(solution)/shard_map/convert_element_type | solution.py:148
  254.1 40.5 %all-to-all-done.3 = bf16[16,32,32,128]{3,2,1,0:T(8,128)(2,1)} async-done(((bf16[16,32,32,128]{3,2,1,0:T(8,128)(2,1)}), bf16[16,32,32,128]{3,2,1,0:T(8,128)(2,1)}, u32[]{:S(2)}, u32[]{:S(2)}) %all-to-all-start.3) | async-done | bytes 4194336 | tf_op jit(solution)/shard_map/all_to_all | solution.py:62
  294.6 6.6 %fusion.3 = bf16[32,512,128]{1,2,0:T(8,128)(2,1)} fusion(bf16[16,32,32,128]{3,2,1,0:T(8,128)(2,1)} %all-to-all-done.3, bf16[512,16,32,1]{0,2,3,1:T(8,128)(2,1)S(1)} %bitcast.108), kind=kOutput, calls=%fused_computation.8 | convolution fusion | flops 2149580800 | bytes 8912896 | tf_op jit(solution)/shard_map/dirc,jdr->ijc/dot_general | solution.py:135
  301.2 6.5 %copy.62 = bf16[32,512,128]{2,1,0:T(8,128)(2,1)} copy(bf16[32,512,128]{1,2,0:T(8,128)(2,1)} %fusion.3) | data formatting | bytes 8388608 | tf_op jit(solution)/shard_map/dirc,jdr->ijc/transpose | solution.py:135
  307.7 5.8 %convolution_bitcast_fusion = f32[512,16,32]{0,2,1:T(8,128)S(1)} fusion(bf16[32,512,128,1]{2,1,0,3:T(8,128)(2,1)} %bitcast.91, bf16[16,32,32,128]{3,2,1,0:T(8,128)(2,1)} %all-to-all-done.3), kind=kOutput, calls=%fused_computation.24 | convolution fusion | flops 2147483648 | bytes 9437184 | tf_op jit(solution)/shard_map/ijc,dirc->jdr/dot_general | solution.py:136
  320.5 7.1 %fusion.23 = f32[128,256]{0,1:T(8,128)S(1)} fusion(bf16[1,16384,128]{2,1,0:T(8,128)(2,1)} %param.7, bf16[16384,128]{1,0:T(8,128)(2,1)} %bitcast.100, bf16[16384,128]{1,0:T(8,128)(2,1)} %bitcast.98), kind=kOutput, calls=%fused_computation.30 | convolution fusion | flops 1090519040 | bytes 12713984 | tf_op jit(solution)/shard_map/dot_general | solution.py:149
  331.7 21.3 %all_to_all.32 = f32[8,304,128]{2,1,0:T(8,128)S(1)} all-to-all(f32[8,304,128]{2,1,0:T(8,128)S(1)} %bitcast.94), channel_id=1, replica_groups={{0,2,4,6,8,10,12,14},{1,3,5,7,9,11,13,15},{16,18,20,22,24,26,28,30},{17..., dimensions={0} | all-to-all | bytes 2490368 | tf_op jit(solution)/shard_map/all_to_all | solution.py:62
  353.4 3.8 collective-permute-done.1
  365.3 4.0 collective-permute-done.3
  374.0 5.5 %copy.56 = bf16[32,16,1,32,128]{4,3,1,0,2:T(8,128)(2,1)} copy(bf16[32,16,1,32,128]{4,3,0,1,2:T(8,128)(2,1)} %bitcast.97) | data formatting | bytes 8388608 | tf_op jit(solution)/shard_map/transpose | solution.py:142
  379.5 10.0 %all-to-all-done.5 = f32[8,304,128]{2,1,0:T(8,128)S(1)} async-done(((f32[8,304,128]{2,1,0:T(8,128)}), f32[8,304,128]{2,1,0:T(8,128)S(1)}, u32[]{:S(2)}, u32[]{:S(2)}) %all-to-all-start.5) | async-done | bytes 1245216 | tf_op jit(solution)/shard_map/all_to_all | solution.py:62
  389.5 4.7 %collective-permute-start.4 = (f32[2432,128]{1,0:T(8,128)S(1)}, f32[2432,128]{1,0:T(8,128)S(1)}, u32[]{:S(2)}, u32[]{:S(2)}) collective-permute-start(f32[2432,128]{1,0:T(8,128)S(1)} %bitcast.92), channel_id=1, source_target_pairs={{0,1},{1,0},{2,3},{3,2},{4,5},{5,4},{6,7},{7,6},{8,9},{9,8},{10,11... | collective-permute-start | bytes 3735560 | tf_op jit(solution)/shard_map/ppermute | solution.py:86
  399.1 7.9 %fusion.1 = bf16[1,16384,128]{2,1,0:T(8,128)(2,1)} fusion(f32[16384,128]{1,0:T(8,128)S(1)} %bitcast.89, bf16[128,256]{1,0:T(8,128)(2,1)S(1)} %copy-done.12, bf16[16384,128]{1,0:T(8,128)(2,1)} %bitcast.101, bf16[16384,128]{1,0:T(8,128)(2,1)} %bitcast.99), kind=kOutput, calls=%fused_computation.3 | convolution fusion | flops 1094713344 | bytes 21037056 | tf_op jit(solution)/shard_map/dot_general | solution.py:151
  (65 shorter events, 58.0 us)
Async XLA Ops:
  0.6 70.9 %copy-start = (bf16[512,512]{1,0:T(8,128)(2,1)S(1)}, bf16[512,512]{1,0:T(8,128)(2,1)}, u32[]{:S(2)}) copy-start(bf16[512,512]{1,0:T(8,128)(2,1)} %param.11) | copy-start | bytes 1572868
  5.4 1.9 copy-start.5
  69.5 2.0 copy-start.3
  85.6 6.0 %copy-start.12 = (bf16[128,256]{1,0:T(8,128)(2,1)S(1)}, bf16[128,256]{1,0:T(8,128)(2,1)}, u32[]{:S(2)}) copy-start(bf16[128,256]{1,0:T(8,128)(2,1)} %param.9) | copy-start | bytes 196612
  85.6 6.6 %copy-start.9 = (bf16[128,256]{1,0:T(8,128)(2,1)S(1)}, bf16[128,256]{1,0:T(8,128)(2,1)}, u32[]{:S(2)}) copy-start(bf16[128,256]{1,0:T(8,128)(2,1)} %wu_ref.1) | copy-start | bytes 196612
  85.6 7.4 %copy-start.10 = (bf16[256,128]{1,0:T(8,128)(2,1)S(1)}, bf16[256,128]{1,0:T(8,128)(2,1)}, u32[]{:S(2)}) copy-start(bf16[256,128]{1,0:T(8,128)(2,1)} %wd_ref.1) | copy-start | bytes 196612
  85.6 56.9 %all-to-all-start.1 = ((bf16[16,32,32,128]{3,2,1,0:T(8,128)(2,1)}), bf16[16,32,32,128]{3,2,1,0:T(8,128)(2,1)}, u32[]{:S(2)}, u32[]{:S(2)}) async-start(bf16[16,32,32,128]{3,2,1,0:T(8,128)(2,1)} %bitcast.88), calls=%async_computation.1 | async-start | bytes 8388608 | tf_op jit(solution)/shard_map/all_to_all | solution.py:62
  93.7 5.5 %copy-start.2 = (bf16[1,16384,128]{2,1,0:T(8,128)(2,1)S(1)}, bf16[1,16384,128]{2,1,0:T(8,128)(2,1)}, u32[]{:S(2)}) copy-start(bf16[1,16384,128]{2,1,0:T(8,128)(2,1)} %param.7) | copy-start | bytes 12582916
  221.6 1.9 copy-start.6
  237.7 6.1 %copy-start.11 = (f32[128,256]{1,0:T(8,128)S(1)}, f32[128,256]{1,0:T(8,128)}, u32[]{:S(2)}) copy-start(f32[128,256]{1,0:T(8,128)} %get-tuple-element.17) | copy-start | bytes 393220
  237.7 56.9 %all-to-all-start.3 = ((bf16[16,32,32,128]{3,2,1,0:T(8,128)(2,1)}), bf16[16,32,32,128]{3,2,1,0:T(8,128)(2,1)}, u32[]{:S(2)}, u32[]{:S(2)}) async-start(bf16[16,32,32,128]{3,2,1,0:T(8,128)(2,1)} %bitcast.87), calls=%async_computation.3 | async-start | bytes 8388608 | tf_op jit(solution)/shard_map/all_to_all | solution.py:62
  243.8 5.6 %copy-start.4 = (bf16[16,32,32,128]{3,2,1,0:T(8,128)(2,1)S(1)}, bf16[16,32,32,128]{3,2,1,0:T(8,128)(2,1)}, u32[]{:S(2)}) copy-start(bf16[16,32,32,128]{3,2,1,0:T(8,128)(2,1)} %copy-done.3) | copy-start | bytes 12582916
  243.8 5.6 %copy-start.7 = (bf16[16,32,32,128]{3,2,1,0:T(8,128)(2,1)S(1)}, bf16[16,32,32,128]{3,2,1,0:T(8,128)(2,1)}, u32[]{:S(2)}) copy-start(bf16[16,32,32,128]{3,2,1,0:T(8,128)(2,1)} %copy-done.6) | copy-start | bytes 12582916
  320.5 7.2 %copy-start.8 = (f32[256,128]{1,0:T(8,128)S(1)}, f32[256,128]{1,0:T(8,128)}, u32[]{:S(2)}) copy-start(f32[256,128]{1,0:T(8,128)} %get-tuple-element.18) | copy-start | bytes 393220
  327.9 3.7 collective-permute-start
  353.0 4.2 %collective-permute-start.1 = (f32[304,128]{1,0:T(8,128)S(1)}, f32[304,128]{1,0:T(8,128)S(1)}, u32[]{:S(2)}, u32[]{:S(2)}) collective-permute-start(f32[304,128]{1,0:T(8,128)S(1)} %reduce_sum.9), channel_id=1, source_target_pairs={{0,16},{16,0},{32,48},{48,32},{64,80},{80,64},{96,112},{112,96},{1... | collective-permute-start | bytes 466952 | tf_op jit(solution)/shard_map/ppermute | solution.py:83
  357.2 4.6 %collective-permute-start.2 = (f32[304,128]{1,0:T(8,128)S(1)}, f32[304,128]{1,0:T(8,128)S(1)}, u32[]{:S(2)}, u32[]{:S(2)}) collective-permute-start(f32[304,128]{1,0:T(8,128)S(1)} %add.22), channel_id=1, source_target_pairs={{0,32},{16,48},{32,0},{48,16},{64,96},{80,112},{96,64},{112,80},{1... | collective-permute-start | bytes 466952 | tf_op jit(solution)/shard_map/ppermute | solution.py:83
  361.8 7.5 %collective-permute-start.3 = (f32[304,128]{1,0:T(8,128)S(1)}, f32[304,128]{1,0:T(8,128)S(1)}, u32[]{:S(2)}, u32[]{:S(2)}) collective-permute-start(f32[304,128]{1,0:T(8,128)S(1)} %add.23), channel_id=1, source_target_pairs={{0,64},{16,80},{32,96},{48,112},{64,0},{80,16},{96,32},{112,48},{1... | collective-permute-start | bytes 466952 | tf_op jit(solution)/shard_map/ppermute | solution.py:83
  370.5 19.1 %all-to-all-start.5 = ((f32[8,304,128]{2,1,0:T(8,128)}), f32[8,304,128]{2,1,0:T(8,128)S(1)}, u32[]{:S(2)}, u32[]{:S(2)}) async-start(f32[8,304,128]{2,1,0:T(8,128)} %broadcast_in_dim.10), calls=%async_computation.5 | async-start | bytes 2490368 | tf_op jit(solution)/shard_map/all_to_all | solution.py:62
  389.5 17.5 %collective-permute-start.4 = (f32[2432,128]{1,0:T(8,128)S(1)}, f32[2432,128]{1,0:T(8,128)S(1)}, u32[]{:S(2)}, u32[]{:S(2)}) collective-permute-start(f32[2432,128]{1,0:T(8,128)S(1)} %bitcast.92), channel_id=1, source_target_pairs={{0,1},{1,0},{2,3},{3,2},{4,5},{5,4},{6,7},{7,6},{8,9},{9,8},{10,11... | collective-permute-start | bytes 3735560 | tf_op jit(solution)/shard_map/ppermute | solution.py:86
  407.4 4.5 %copy-start.1 = (bf16[512,512]{1,0:T(8,128)(2,1)S(1)}, bf16[512,512]{1,0:T(8,128)(2,1)}, u32[]{:S(2)}) copy-start(bf16[512,512]{1,0:T(8,128)(2,1)} %param.11) | copy-start | bytes 1572868

commit v5 on v4

--- a/solution.py
+++ b/solution.py
@@ -39,7 +39,7 @@
     dm_ref[...] = (dh32 * gate).astype(bf16)
     dg_ref[...] = (dh32 * mixed32 * gate * (1.0 - gate)).astype(bf16)
 
-def mlp(x, cot, mixed, w_gate, w_up, w_down, tile=2048):
+def mlp(x, cot, mixed, w_gate, w_up, w_down, tile=512):
     rows, width = x.shape
     ff = w_up.shape[1]
     f32 = jnp.float32

time: 420 us -> 427 us (1.017); the launches traced: 412 us -> 425 us
  Pallas kernels: 24 us -> 37.2 us
    pallas_call x1, Pallas kernels: 24 us -> 37.2 us  [mlp(): pl.pallas_call(mlp_kernel, grid=(rows // tile,), in_specs=[row, row, row,...]
where the time goes in v5:
time: 427 us; the launch traced here: 425 us
  blocking collectives  135 us (32%)
  waiting for transfers between devices  104 us (24%)
  local copies, waits for them, and re-layouts  67.7 us (16%)
  matrix products  49 us (11%)
  Pallas kernels  37.2 us (9%)
  starting transfers between devices  26.6 us (6%)
    all_to_all x3, blocking collectives, a2a(): return lax.all_to_all(x, axis, 0, 0, tiled=True, axis_index_groups=groups)  135 us
    all_to_all x3, waiting for transfers between devices, a2a(): return lax.all_to_all(x, axis, 0, 0, tiled=True, axis_index_groups=groups)  91.1 us
    pallas_call x1, Pallas kernels, mlp(): pl.pallas_call(mlp_kernel, grid=(rows // tile,), in_specs=[row, row, row,...  37.2 us
    all_to_all x3, starting transfers between devices, a2a(): return lax.all_to_all(x, axis, 0, 0, tiled=True, axis_index_groups=groups)  14.9 us
    ppermute x3, waiting for transfers between devices, all_reduce_a2a(): c = c + lax.ppermute(c, 'dp', [(i, i ^ step) for i in range(n_dp)])  10.4 us
    unnamed x29, local copies, waits for them, and re-layouts  8.72 us
  transfers between devices with their start and end apart: 8, of which 7 were waited for; matrix products, arithmetic and copies ran while one was open for 9% of the time, Pallas kernels for 0%

profile of v5, /device:TPU:1, one launch (start us, length us, event | category | flops | bytes accessed | tf_op | source)
XLA Modules:
  0.0 424.9 jit_solution(14354064419924493677)
XLA Ops:
  10.8 58.7 %all_to_all.30 = bf16[16,32,32,128]{3,2,1,0:T(8,128)(2,1)S(1)} all-to-all(bf16[16,32,32,128]{3,2,1,0:T(8,128)(2,1)S(1)} %copy.51), channel_id=1, replica_groups=mesh['dp'=8,'ctx'=16] {'ctx'}, dimensions={0} | all-to-all | bytes 8388608 | tf_op jit(solution)/shard_map/all_to_all | solution.py:62
  71.5 6.1 %convert_bitcast_fusion.2 = bf16[512,32,128]{0,2,1:T(8,128)(2,1)} fusion(bf16[512,32,128]{2,1,0:T(8,128)(2,1)S(1)} %bitcast.85, bf16[512,512]{1,0:T(8,128)(2,1)S(1)} %copy-done), kind=kOutput, calls=%fused_computation.12 | convolution fusion | flops 2149580800 | bytes 8912896 | tf_op jit(solution)/shard_map/ikc,im->mkc/dot_general | solution.py:120
  77.6 8.0 %copy.53 = bf16[512,32,128]{2,1,0:T(8,128)(2,1)} copy(bf16[512,32,128]{0,2,1:T(8,128)(2,1)} %convert_bitcast_fusion.2) | data formatting | bytes 8388608 | tf_op jit(solution)/shard_map/convert_element_type | solution.py:120
  85.6 5.7 %all-to-all-start.1 = ((bf16[16,32,32,128]{3,2,1,0:T(8,128)(2,1)}), bf16[16,32,32,128]{3,2,1,0:T(8,128)(2,1)}, u32[]{:S(2)}, u32[]{:S(2)}) async-start(bf16[16,32,32,128]{3,2,1,0:T(8,128)(2,1)} %bitcast.88), calls=%async_computation.1 | async-start | bytes 8388608 | tf_op jit(solution)/shard_map/all_to_all | solution.py:62
  93.4 5.5 %copy.49 = bf16[32,16,32,128]{3,2,0,1:T(8,128)(2,1)} copy(bf16[32,16,32,128]{3,2,1,0:T(8,128)(2,1)} %bitcast.96) | data formatting | bytes 8388608 | tf_op jit(solution)/shard_map/squeeze;reshape;squeeze | solution.py:124
  102.0 40.3 %all-to-all-done.1 = bf16[16,32,32,128]{3,2,1,0:T(8,128)(2,1)} async-done(((bf16[16,32,32,128]{3,2,1,0:T(8,128)(2,1)}), bf16[16,32,32,128]{3,2,1,0:T(8,128)(2,1)}, u32[]{:S(2)}, u32[]{:S(2)}) %all-to-all-start.1) | async-done | bytes 4194336 | tf_op jit(solution)/shard_map/all_to_all | solution.py:62
  142.3 37.2 %shard_map.126 = (bf16[16384,128]{1,0:T(8,128)(2,1)}, bf16[16384,128]{1,0:T(8,128)(2,1)}, bf16[16384,128]{1,0:T(8,128)(2,1)}, bf16[16384,128]{1,0:T(8,128)(2,1)}...) custom-call(bf16[16384,128]{1,0:T(8,128)(2,1)} %bitcast.84, bf16[16384,128]{1,0:T(8,128)(2,1)} %bitcast.83, ...), custom_call_target="tpu_custom_call" | custom-call | tf_op jit(solution)/shard_map/pallas_call | solution.py:49
  179.6 55.3 %all_to_all.31 = bf16[16,32,32,128]{3,2,1,0:T(8,128)(2,1)S(1)} all-to-all(bf16[16,32,32,128]{3,2,1,0:T(8,128)(2,1)} %bitcast.106), channel_id=1, replica_groups=mesh['dp'=8,'ctx'=16] {'ctx'}, dimensions={0} | all-to-all | bytes 8388608 | tf_op jit(solution)/shard_map/all_to_all | solution.py:62
  236.8 6.4 %convert_bitcast_fusion.1 = bf16[512,32,128]{0,2,1:T(8,128)(2,1)} fusion(bf16[512,32,128]{2,1,0:T(8,128)(2,1)S(1)} %bitcast.104, bf16[512,512]{1,0:T(8,128)(2,1)S(1)} %copy-done), kind=kOutput, calls=%fused_computation.11 | convolution fusion | flops 2149580800 | bytes 8912896 | tf_op jit(solution)/shard_map/mkc,im->ikc/dot_general | solution.py:130
  243.2 7.8 %copy.60 = bf16[512,32,128]{2,1,0:T(8,128)(2,1)} copy(bf16[512,32,128]{0,2,1:T(8,128)(2,1)} %convert_bitcast_fusion.1) | data formatting | bytes 8388608 | tf_op jit(solution)/shard_map/convert_element_type | solution.py:130
  251.0 5.7 %all-to-all-start.3 = ((bf16[16,32,32,128]{3,2,1,0:T(8,128)(2,1)}), bf16[16,32,32,128]{3,2,1,0:T(8,128)(2,1)}, u32[]{:S(2)}, u32[]{:S(2)}) async-start(bf16[16,32,32,128]{3,2,1,0:T(8,128)(2,1)} %bitcast.87), calls=%async_computation.3 | async-start | bytes 8388608 | tf_op jit(solution)/shard_map/all_to_all | solution.py:62
  256.7 5.5 %copy.58 = bf16[16,32,1,32,128]{4,3,0,1,2:T(8,128)(2,1)} copy(bf16[16,32,1,32,128]{4,3,1,0,2:T(8,128)(2,1)} %bitcast.102) | data formatting | bytes 8388608 | tf_op jit(solution)/shard_map/convert_element_type | solution.py:148
  267.0 40.7 %all-to-all-done.3 = bf16[16,32,32,128]{3,2,1,0:T(8,128)(2,1)} async-done(((bf16[16,32,32,128]{3,2,1,0:T(8,128)(2,1)}), bf16[16,32,32,128]{3,2,1,0:T(8,128)(2,1)}, u32[]{:S(2)}, u32[]{:S(2)}) %all-to-all-start.3) | async-done | bytes 4194336 | tf_op jit(solution)/shard_map/all_to_all | solution.py:62
  307.7 6.6 %fusion.3 = bf16[32,512,128]{1,2,0:T(8,128)(2,1)} fusion(bf16[16,32,32,128]{3,2,1,0:T(8,128)(2,1)} %all-to-all-done.3, bf16[512,16,32,1]{0,2,3,1:T(8,128)(2,1)S(1)} %bitcast.108), kind=kOutput, calls=%fused_computation.8 | convolution fusion | flops 2149580800 | bytes 8912896 | tf_op jit(solution)/shard_map/dirc,jdr->ijc/dot_general | solution.py:135
  314.3 6.5 %copy.62 = bf16[32,512,128]{2,1,0:T(8,128)(2,1)} copy(bf16[32,512,128]{1,2,0:T(8,128)(2,1)} %fusion.3) | data formatting | bytes 8388608 | tf_op jit(solution)/shard_map/dirc,jdr->ijc/transpose | solution.py:135
  320.8 5.8 %convolution_bitcast_fusion = f32[512,16,32]{0,2,1:T(8,128)S(1)} fusion(bf16[32,512,128,1]{2,1,0,3:T(8,128)(2,1)} %bitcast.91, bf16[16,32,32,128]{3,2,1,0:T(8,128)(2,1)} %all-to-all-done.3), kind=kOutput, calls=%fused_computation.24 | convolution fusion | flops 2147483648 | bytes 9437184 | tf_op jit(solution)/shard_map/ijc,dirc->jdr/dot_general | solution.py:136
  333.6 7.1 %fusion.23 = f32[128,256]{0,1:T(8,128)S(1)} fusion(bf16[1,16384,128]{2,1,0:T(8,128)(2,1)} %param.7, bf16[16384,128]{1,0:T(8,128)(2,1)} %bitcast.100, bf16[16384,128]{1,0:T(8,128)(2,1)} %bitcast.98), kind=kOutput, calls=%fused_computation.30 | convolution fusion | flops 1090519040 | bytes 12713984 | tf_op jit(solution)/shard_map/dot_general | solution.py:149
  344.8 21.3 %all_to_all.32 = f32[8,304,128]{2,1,0:T(8,128)S(1)} all-to-all(f32[8,304,128]{2,1,0:T(8,128)S(1)} %bitcast.94), channel_id=1, replica_groups={{0,2,4,6,8,10,12,14},{1,3,5,7,9,11,13,15},{16,18,20,22,24,26,28,30},{17..., dimensions={0} | all-to-all | bytes 2490368 | tf_op jit(solution)/shard_map/all_to_all | solution.py:62
  366.5 3.8 collective-permute-done.1
  378.4 4.0 collective-permute-done.3
  387.1 5.5 %copy.56 = bf16[32,16,1,32,128]{4,3,1,0,2:T(8,128)(2,1)} copy(bf16[32,16,1,32,128]{4,3,0,1,2:T(8,128)(2,1)} %bitcast.97) | data formatting | bytes 8388608 | tf_op jit(solution)/shard_map/transpose | solution.py:142
  392.6 10.0 %all-to-all-done.5 = f32[8,304,128]{2,1,0:T(8,128)S(1)} async-done(((f32[8,304,128]{2,1,0:T(8,128)}), f32[8,304,128]{2,1,0:T(8,128)S(1)}, u32[]{:S(2)}, u32[]{:S(2)}) %all-to-all-start.5) | async-done | bytes 1245216 | tf_op jit(solution)/shard_map/all_to_all | solution.py:62
  402.6 4.7 %collective-permute-start.4 = (f32[2432,128]{1,0:T(8,128)S(1)}, f32[2432,128]{1,0:T(8,128)S(1)}, u32[]{:S(2)}, u32[]{:S(2)}) collective-permute-start(f32[2432,128]{1,0:T(8,128)S(1)} %bitcast.92), channel_id=1, source_target_pairs={{0,1},{1,0},{2,3},{3,2},{4,5},{5,4},{6,7},{7,6},{8,9},{9,8},{10,11... | collective-permute-start | bytes 3735560 | tf_op jit(solution)/shard_map/ppermute | solution.py:86
  412.1 7.9 %fusion.1 = bf16[1,16384,128]{2,1,0:T(8,128)(2,1)} fusion(f32[16384,128]{1,0:T(8,128)S(1)} %bitcast.89, bf16[128,256]{1,0:T(8,128)(2,1)S(1)} %copy-done.12, bf16[16384,128]{1,0:T(8,128)(2,1)} %bitcast.101, bf16[16384,128]{1,0:T(8,128)(2,1)} %bitcast.99), kind=kOutput, calls=%fused_computation.3 | convolution fusion | flops 1094713344 | bytes 21037056 | tf_op jit(solution)/shard_map/dot_general | solution.py:151
  (65 shorter events, 58.0 us)
Async XLA Ops:
  0.6 70.9 %copy-start = (bf16[512,512]{1,0:T(8,128)(2,1)S(1)}, bf16[512,512]{1,0:T(8,128)(2,1)}, u32[]{:S(2)}) copy-start(bf16[512,512]{1,0:T(8,128)(2,1)} %param.11) | copy-start | bytes 1572868
  5.4 1.9 copy-start.5
  69.5 2.0 copy-start.3
  85.6 5.7 %copy-start.12 = (bf16[128,256]{1,0:T(8,128)(2,1)S(1)}, bf16[128,256]{1,0:T(8,128)(2,1)}, u32[]{:S(2)}) copy-start(bf16[128,256]{1,0:T(8,128)(2,1)} %param.9) | copy-start | bytes 196612
  85.6 6.3 %copy-start.9 = (bf16[128,256]{1,0:T(8,128)(2,1)S(1)}, bf16[128,256]{1,0:T(8,128)(2,1)}, u32[]{:S(2)}) copy-start(bf16[128,256]{1,0:T(8,128)(2,1)} %wu_ref.1) | copy-start | bytes 196612
  85.6 7.1 %copy-start.10 = (bf16[256,128]{1,0:T(8,128)(2,1)S(1)}, bf16[256,128]{1,0:T(8,128)(2,1)}, u32[]{:S(2)}) copy-start(bf16[256,128]{1,0:T(8,128)(2,1)} %wd_ref.1) | copy-start | bytes 196612
  85.6 56.7 %all-to-all-start.1 = ((bf16[16,32,32,128]{3,2,1,0:T(8,128)(2,1)}), bf16[16,32,32,128]{3,2,1,0:T(8,128)(2,1)}, u32[]{:S(2)}, u32[]{:S(2)}) async-start(bf16[16,32,32,128]{3,2,1,0:T(8,128)(2,1)} %bitcast.88), calls=%async_computation.1 | async-start | bytes 8388608 | tf_op jit(solution)/shard_map/all_to_all | solution.py:62
  93.4 5.5 %copy-start.2 = (bf16[1,16384,128]{2,1,0:T(8,128)(2,1)S(1)}, bf16[1,16384,128]{2,1,0:T(8,128)(2,1)}, u32[]{:S(2)}) copy-start(bf16[1,16384,128]{2,1,0:T(8,128)(2,1)} %param.7) | copy-start | bytes 12582916
  234.9 1.9 copy-start.6
  251.0 5.7 %copy-start.11 = (f32[128,256]{1,0:T(8,128)S(1)}, f32[128,256]{1,0:T(8,128)}, u32[]{:S(2)}) copy-start(f32[128,256]{1,0:T(8,128)} %get-tuple-element.17) | copy-start | bytes 393220
  251.0 56.7 %all-to-all-start.3 = ((bf16[16,32,32,128]{3,2,1,0:T(8,128)(2,1)}), bf16[16,32,32,128]{3,2,1,0:T(8,128)(2,1)}, u32[]{:S(2)}, u32[]{:S(2)}) async-start(bf16[16,32,32,128]{3,2,1,0:T(8,128)(2,1)} %bitcast.87), calls=%async_computation.3 | async-start | bytes 8388608 | tf_op jit(solution)/shard_map/all_to_all | solution.py:62
  256.7 5.6 %copy-start.4 = (bf16[16,32,32,128]{3,2,1,0:T(8,128)(2,1)S(1)}, bf16[16,32,32,128]{3,2,1,0:T(8,128)(2,1)}, u32[]{:S(2)}) copy-start(bf16[16,32,32,128]{3,2,1,0:T(8,128)(2,1)} %copy-done.3) | copy-start | bytes 12582916
  256.7 5.6 %copy-start.7 = (bf16[16,32,32,128]{3,2,1,0:T(8,128)(2,1)S(1)}, bf16[16,32,32,128]{3,2,1,0:T(8,128)(2,1)}, u32[]{:S(2)}) copy-start(bf16[16,32,32,128]{3,2,1,0:T(8,128)(2,1)} %copy-done.6) | copy-start | bytes 12582916
  333.6 7.2 %copy-start.8 = (f32[256,128]{1,0:T(8,128)S(1)}, f32[256,128]{1,0:T(8,128)}, u32[]{:S(2)}) copy-start(f32[256,128]{1,0:T(8,128)} %get-tuple-element.18) | copy-start | bytes 393220
  341.0 3.7 collective-permute-start
  366.1 4.2 collective-permute-start.1
  370.3 4.5 %collective-permute-start.2 = (f32[304,128]{1,0:T(8,128)S(1)}, f32[304,128]{1,0:T(8,128)S(1)}, u32[]{:S(2)}, u32[]{:S(2)}) collective-permute-start(f32[304,128]{1,0:T(8,128)S(1)} %add.22), channel_id=1, source_target_pairs={{0,32},{16,48},{32,0},{48,16},{64,96},{80,112},{96,64},{112,80},{1... | collective-permute-start | bytes 466952 | tf_op jit(solution)/shard_map/ppermute | solution.py:83
  374.9 7.5 %collective-permute-start.3 = (f32[304,128]{1,0:T(8,128)S(1)}, f32[304,128]{1,0:T(8,128)S(1)}, u32[]{:S(2)}, u32[]{:S(2)}) collective-permute-start(f32[304,128]{1,0:T(8,128)S(1)} %add.23), channel_id=1, source_target_pairs={{0,64},{16,80},{32,96},{48,112},{64,0},{80,16},{96,32},{112,48},{1... | collective-permute-start | bytes 466952 | tf_op jit(solution)/shard_map/ppermute | solution.py:83
  383.5 19.1 %all-to-all-start.5 = ((f32[8,304,128]{2,1,0:T(8,128)}), f32[8,304,128]{2,1,0:T(8,128)S(1)}, u32[]{:S(2)}, u32[]{:S(2)}) async-start(f32[8,304,128]{2,1,0:T(8,128)} %broadcast_in_dim.10), calls=%async_computation.5 | async-start | bytes 2490368 | tf_op jit(solution)/shard_map/all_to_all | solution.py:62
  402.6 17.5 %collective-permute-start.4 = (f32[2432,128]{1,0:T(8,128)S(1)}, f32[2432,128]{1,0:T(8,128)S(1)}, u32[]{:S(2)}, u32[]{:S(2)}) collective-permute-start(f32[2432,128]{1,0:T(8,128)S(1)} %bitcast.92), channel_id=1, source_target_pairs={{0,1},{1,0},{2,3},{3,2},{4,5},{5,4},{6,7},{7,6},{8,9},{9,8},{10,11... | collective-permute-start | bytes 3735560 | tf_op jit(solution)/shard_map/ppermute | solution.py:86
  420.4 4.5 %copy-start.1 = (bf16[512,512]{1,0:T(8,128)(2,1)S(1)}, bf16[512,512]{1,0:T(8,128)(2,1)}, u32[]{:S(2)}) copy-start(bf16[512,512]{1,0:T(8,128)(2,1)} %param.11) | copy-start | bytes 1572868
